TPU v7x, 128 devices: a whole 4x4x4 slice. The times are simulated.
128 devices in a mesh: replica: 8 (over z, y_lo), fsdp: 16 (over y_hi, x, core).
Axes of the slice: x: 4, y: 4 (y_hi: 2, y_lo: 2; y = y_hi * 2 + y_lo), z: 4, core: 2. Of those that a mesh axis runs over, the one named last changes fastest.
Arguments:
- tokens: bfloat16 [8, 2048, 4096], P('replica', 'fsdp'), may hold values from -6 to 6
- queries: bfloat16 [8, 2048, 4096], P('replica', 'fsdp'), may hold values from -64 to 64
- keys: bfloat16 [8, 2048, 512], P('replica', 'fsdp'), may hold values from -4 to 4
- value_weight: bfloat16 [4096, 512], P('fsdp'), may hold values from -4 to 4
- ctx_grad: bfloat16 [8, 2048, 4096], P('replica', 'fsdp'), may hold values from -6 to 6
- frag_global: float32 [4096, 2048], P('fsdp', 'replica'), may hold values from -4 to 4
- frag_momentum: float32 [4096, 2048], P('fsdp', 'replica'), may hold values from -1.8 to 1.8
- frag_local: bfloat16 [8, 4096, 2048], P('replica', 'fsdp'), may hold values from -6 to 6
Outputs:
- context: bfloat16 [8, 2048, 4096], P('replica', 'fsdp')
- query_grad: bfloat16 [8, 2048, 4096], P('replica', 'fsdp')
- key_grad: bfloat16 [8, 2048, 512], P('replica', 'fsdp')
- weight_grad: float32 [8, 4096, 512], P('replica', 'fsdp')
- token_grad: bfloat16 [8, 2048, 4096], P('replica', 'fsdp')
- new_global: float32 [4096, 2048], P('fsdp', 'replica')
- new_momentum: float32 [4096, 2048], P('fsdp', 'replica')
- refreshed_local: bfloat16 [4096, 2048], P('fsdp')
All inputs are finite; a program needn't handle non-finite values.
Results may differ from a plain program's by a relative error of at most 0.02.
Values may be sent and summed in bfloat16 or wider, within the bound.
No kernel may reach another device: no remote copies, remote signals or barrier semaphores. Data moves between devices by JAX's collectives and lax.ppermute only.
A program may use at most 192 MiB of HBM per device.

v0:
```python
import jax
import jax.numpy as jnp
from jax import lax
from jax.sharding import PartitionSpec as P

HD = 128


outer_momentum = 0.9
outer_rate = 0.7
masked_score = -1e30


def on_device(
    tokens, queries, keys, value_weight, ctx_grad, frag_global, frag_momentum, frag_local
):
    tokens = tokens[0]
    queries = queries[0]
    keys = keys[0]
    ctx_grad = ctx_grad[0]
    tok_rows = tokens.shape[0]
    model_width = tokens.shape[1]
    proj_scale = model_width ** (-0.5)
    score_scale = HD ** (-0.5)
    kv_heads = keys.shape[1] // HD
    group = queries.shape[1] // (kv_heads * HD)
    key_rows = keys.shape[0]
    weight_rows = value_weight.shape[0]
    fsdp_size = lax.axis_size("fsdp")
    gathered = lax.all_gather(
        jnp.concatenate([keys, value_weight], axis=0), "fsdp", axis=0, tiled=False
    )
    keys_all = gathered[:, :key_rows].reshape(fsdp_size * key_rows, keys.shape[1])
    weight_all = gathered[:, key_rows:].reshape(fsdp_size * weight_rows, value_weight.shape[1])
    replicas = lax.axis_size("replica")
    share_cols = frag_global.shape[1]
    frag_rows = frag_global.shape[0]
    local_parts = lax.all_to_all(
        frag_local[0].reshape(frag_rows, replicas, share_cols).transpose(1, 0, 2),
        "replica",
        0,
        0,
        tiled=True,
    )
    own_sum = jnp.sum(local_parts.astype(jnp.float32), axis=0)
    delta = frag_global - own_sum / replicas
    new_momentum = outer_momentum * frag_momentum + delta
    new_global = frag_global - outer_rate * (delta + outer_momentum * new_momentum)
    refreshed_parts = lax.all_to_all(
        jnp.broadcast_to(
            new_global.astype(jnp.bfloat16)[None], (replicas, frag_rows, share_cols)
        ),
        "replica",
        0,
        0,
        tiled=True,
    )
    refreshed_local = refreshed_parts.transpose(1, 0, 2).reshape(frag_rows, replicas * share_cols)
    refreshed_local, keys_all = lax.optimization_barrier((refreshed_local, keys_all))
    value_sum = jnp.dot(tokens, weight_all, preferred_element_type=jnp.float32)
    values = (value_sum * proj_scale).astype(jnp.bfloat16)
    values_all = lax.all_gather(values, "fsdp", axis=0, tiled=True)
    length_all = keys_all.shape[0]
    query_pos = lax.axis_index("fsdp") * tok_rows + jnp.arange(tok_rows)
    causal = jnp.arange(length_all)[None, :] <= query_pos[:, None]
    query_heads = queries.reshape(tok_rows, kv_heads, group, HD)
    grad_heads = ctx_grad.reshape(tok_rows, kv_heads, group, HD)
    key_groups = keys_all.reshape(length_all, kv_heads, HD)
    scores = (
        jnp.einsum("tghd,sgd->ghts", query_heads, key_groups, preferred_element_type=jnp.float32)
        * score_scale
    )
    scores = jnp.where(causal[None, None], scores, masked_score)
    top = jnp.max(scores, axis=-1, keepdims=True)
    summed = jnp.sum(jnp.exp(scores - top), axis=-1, keepdims=True)
    log_total = top + jnp.log(summed)
    probs = jnp.exp(scores - log_total)
    probs_low = probs.astype(jnp.bfloat16)
    value_term = (
        jnp.einsum("ghts,tghd->sgd", probs_low, grad_heads, preferred_element_type=jnp.float32)
        .reshape(length_all, kv_heads * HD)
        .astype(jnp.bfloat16)
    )
    value_term, values_all = lax.optimization_barrier((value_term, values_all))
    kv_width = value_term.shape[1]
    value_parts = lax.all_to_all(
        value_term.reshape(fsdp_size, tok_rows, kv_width), "fsdp", 0, 0, tiled=True
    )
    value_grad = jnp.sum(value_parts.astype(jnp.float32), axis=0).astype(jnp.bfloat16)
    value_groups = values_all.reshape(length_all, kv_heads, HD)
    context_heads = jnp.einsum(
        "ghts,sgd->tghd", probs_low, value_groups, preferred_element_type=jnp.float32
    ).astype(jnp.bfloat16)
    dprobs = jnp.einsum(
        "tghd,sgd->ghts", grad_heads, value_groups, preferred_element_type=jnp.float32
    )
    rowdot = jnp.sum(
        grad_heads.astype(jnp.float32) * context_heads.astype(jnp.float32), axis=-1
    ).transpose(1, 2, 0)[..., None]
    dscores = (probs * (dprobs - rowdot) * score_scale).astype(jnp.bfloat16)
    query_grad = (
        jnp.einsum("ghts,sgd->tghd", dscores, key_groups, preferred_element_type=jnp.float32)
        .astype(jnp.bfloat16)
        .reshape(tok_rows, queries.shape[1])
    )
    key_term = (
        jnp.einsum("ghts,tghd->sgd", dscores, query_heads, preferred_element_type=jnp.float32)
        .reshape(length_all, kv_width)
        .astype(jnp.bfloat16)
    )
    context = context_heads.reshape(tok_rows, queries.shape[1])
    key_parts = lax.all_to_all(
        key_term.reshape(fsdp_size, tok_rows, kv_width), "fsdp", 0, 0, tiled=True
    )
    key_grad = jnp.sum(key_parts.astype(jnp.float32), axis=0).astype(jnp.bfloat16)
    product = lax.dot_general(
        tokens, value_grad, (((0,), (0,)), ((), ())), preferred_element_type=jnp.float32
    )
    weight_term = (product * proj_scale).astype(jnp.bfloat16)
    weight_grad = lax.psum_scatter(
        weight_term, "fsdp", scatter_dimension=0, tiled=True
    ).astype(jnp.float32)
    token_sum = lax.dot_general(
        value_grad,
        weight_all,
        (((1,), (1,)), ((), ())),
        preferred_element_type=jnp.float32,
    )
    token_grad = (token_sum * proj_scale).astype(jnp.bfloat16)
    return (
        context[None],
        query_grad[None],
        key_grad[None],
        weight_grad[None],
        token_grad[None],
        new_global,
        new_momentum,
        refreshed_local,
    )


def solution(mesh):
    return jax.shard_map(
        on_device,
        mesh=mesh,
        in_specs=(
            P("replica", "fsdp", None),
            P("replica", "fsdp", None),
            P("replica", "fsdp", None),
            P("fsdp", None),
            P("replica", "fsdp", None),
            P("fsdp", "replica"),
            P("fsdp", "replica"),
            P("replica", "fsdp", None),
        ),
        out_specs=(
            P("replica", "fsdp", None),
            P("replica", "fsdp", None),
            P("replica", "fsdp", None),
            P("replica", "fsdp", None),
            P("replica", "fsdp", None),
            P("fsdp", "replica"),
            P("fsdp", "replica"),
            P("fsdp", None),
        ),
        check_vma=False,
    )
```

profile of v0, /device:TPU:1, one launch (start us, length us, event | category | flops | bytes accessed | tf_op | source)
XLA Modules:
  0.0 305.1 jit_solution(16680458314097165906)
XLA Ops:
  11.1 24.6 %all_to_all.20 = bf16[8,256,256]{2,1,0:T(8,128)(2,1)S(1)} all-to-all(bf16[8,256,256]{2,1,0:T(8,128)(2,1)S(1)} %copy.62), channel_id=1, replica_groups=mesh['replica'=8,'fsdp'=16] {'replica'}, dimensions={0} | all-to-all | bytes 2097152 | tf_op jit(solution)/shard_map/all_to_all | solution.py:38
  35.8 1.9 fusion.22
  38.7 3.6 %all-to-all-start.1 = ((bf16[8,256,256]{2,1,0:T(8,128)(2,1)}), bf16[8,256,256]{2,1,0:T(8,128)(2,1)S(1)}, u32[]{:S(2)}, u32[]{:S(2)}) async-start(bf16[8,256,256]{2,1,0:T(8,128)(2,1)} %broadcast_in_dim.37), calls=%async_computation.1 | async-start | bytes 2097152 | tf_op jit(solution)/shard_map/all_to_all | solution.py:49
  42.4 2.4 copy.101
  44.8 2.3 copy.67
  47.2 8.4 %all-to-all-done.1 = bf16[8,256,256]{2,1,0:T(8,128)(2,1)S(1)} async-done(((bf16[8,256,256]{2,1,0:T(8,128)(2,1)}), bf16[8,256,256]{2,1,0:T(8,128)(2,1)S(1)}, u32[]{:S(2)}, u32[]{:S(2)}) %all-to-all-start.1) | async-done | bytes 1048608 | tf_op jit(solution)/shard_map/all_to_all | solution.py:49
  57.0 28.6 %all-gather.6.cloned.1.call-done = bf16[6144,512]{1,0:T(8,128)(2,1)} async-done(((bf16[384,512]{1,0:T(8,128)(2,1)}), bf16[6144,512]{1,0:T(8,128)(2,1)}) %all-gather.6.cloned.1.call-update) | async-done | bytes 6291472 | tf_op jit(solution)/shard_map/all_gather | solution.py:30
  85.6 3.1 %slice.8 = bf16[16,128,512]{2,1,0:T(8,128)(2,1)} slice(bf16[16,384,512]{2,1,0:T(8,128)(2,1)} %bitcast.115), slice={[0:16], [0:128], [0:512]} | slice | bytes 4194304 | tf_op jit(solution)/shard_map/slice | solution.py:33
  88.7 4.6 %slice.9 = bf16[16,256,512]{2,1,0:T(8,128)(2,1)} slice(bf16[16,384,512]{2,1,0:T(8,128)(2,1)} %bitcast.116), slice={[0:16], [128:384], [0:512]} | slice | bytes 8388608 | tf_op jit(solution)/shard_map/slice | solution.py:34
  93.3 2.9 copy.64
  96.3 4.1 %fusion.10 = bf16[128,512]{0,1:T(8,128)(2,1)} fusion(bf16[4096,512]{1,0:T(8,128)(2,1)} %bitcast.109, bf16[1,128,4096]{2,1,0:T(8,128)(2,1)S(1)} %copy-done), kind=kOutput, calls=%fused_computation.23 | convolution fusion | flops 537001984 | bytes 5373952 | tf_op jit(solution)/shard_map/dot_general | solution.py:60
  100.7 15.1 %fusion.4 = (f32[4,8,128]{2,1,0:T(8,128)S(1)}, f32[4,2048,128,8]{2,1,3,0:T(8,128)}) fusion(pred[128,2048]{0,1:T(8,128)(4,1)S(1)} %iota_compare_fusion, bf16[2048,4,128,1]{0,2,3,1:T(8,128)(2,1)S(1)} %bitcast.107, bf16[128,4,8,128]{3,2,1,0:T(8,128)(2,1)} %bitcast.117), kind=kOutput, calls=%fused_computation.8 | convolution fusion | flops 2172645376 | bytes 36978688 | tf_op jit(solution)/shard_map/tghd,sgd->ghts/dot_general | solution.py:70
  115.7 14.3 %exponential_reduce_fusion = f32[4,8,128]{2,1,0:T(8,128)S(1)} fusion(f32[4,2048,128,8]{2,1,3,0:T(8,128)} %get-tuple-element.52, f32[4,8,128]{2,1,0:T(8,128)S(1)} %get-tuple-element.51, pred[128,2048]{0,1:T(8,128)(4,1)S(1)} %iota_compare_fusion), kind=kLoop, calls=%fused_computation.6 | loop fusion | flops 33550336 | bytes 33849344 | tf_op jit(solution)/shard_map/reduce_sum | solution.py:75
  130.0 16.1 %bitcast_convert_fusion.1 = bf16[4,2048,128]{1,2,0:T(8,128)(2,1)} fusion(bf16[128,4,8,128]{0,3,2,1:T(8,128)(2,1)} %bitcast.124, f32[4,2048,128,8]{2,1,3,0:T(8,128)} %get-tuple-element.52, f32[4,8,128]{2,1,0:T(8,128)S(1)} %log_add_fusion, pred[128,2048]{0,1:T(8,128)(4,1)S(1)} %iota_compare_fusion), kind=kOutput, calls=%fused_computation.15 | convolution fusion | flops 2182086656 | bytes 36978688 | tf_op jit(solution)/shard_map/ghts,tghd->sgd/dot_general | solution.py:80
  146.1 2.3 all-gather.4.cloned.1.call-done
  148.4 3.9 %copy.77 = bf16[2048,512]{1,0:T(8,128)(2,1)} copy(bf16[2048,512]{0,1:T(8,128)(2,1)} %bitcast.122) | data formatting | bytes 4194304 | tf_op jit(solution)/shard_map/optimization_barrier | solution.py:84
  152.3 3.9 %copy.78 = bf16[16,128,512]{1,2,0:T(8,128)(2,1)} copy(bf16[16,128,512]{2,1,0:T(8,128)(2,1)} %bitcast.112) | data formatting | bytes 4194304 | tf_op jit(solution)/shard_map/reshape | solution.py:87
  156.2 32.5 %all_to_all.21 = bf16[16,128,512]{1,2,0:T(8,128)(2,1)} all-to-all(bf16[16,128,512]{1,2,0:T(8,128)(2,1)} %copy.78), channel_id=1, replica_groups=mesh['replica'=8,'fsdp'=16] {'fsdp'}, dimensions={0} | all-to-all | bytes 4194304 | tf_op jit(solution)/shard_map/all_to_all | solution.py:86
  188.7 1.9 reduce_sum.55
  190.6 3.2 %fusion.5 = bf16[4096,512]{0,1:T(8,128)(2,1)} fusion(bf16[128,512]{0,1:T(8,128)(2,1)S(1)} %reduce_sum.55, bf16[1,128,4096]{2,1,0:T(8,128)(2,1)S(1)} %copy-done), kind=kOutput, calls=%fused_computation.10 | convolution fusion | flops 541065216 | bytes 5373952 | tf_op jit(solution)/shard_map/dot_general | solution.py:116
  193.8 17.5 %multiply_reduce_fusion = (f32[128,4,8]{0,2,1:T(8,128)S(1)}, bf16[4,128,8,128]{3,1,2,0:T(8,128)(2,1)}) fusion(bf16[128,4,8,128]{0,3,2,1:T(8,128)(2,1)} %bitcast.125, bf16[2048,4,128,1]{0,2,3,1:T(8,128)(2,1)} %bitcast.130, f32[4,2048,128,8]{2,1,3,0:T(8,128)} %get-tuple-element.52, f32[4,8,128]{2,1,0:T(8,128)S(1)} %log_add_fusion, ...), kind=kOutput, calls=%fused_computation.17 | convolution fusion | flops 2183655424 | bytes 38043648 | tf_op jit(solution)/shard_map/ghts,sgd->tghd/dot_general | solution.py:91
  211.3 22.5 %fusion.2 = bf16[4,8,128,2048]{2,3,1,0:T(8,128)(2,1)} fusion(f32[4,2048,128,8]{2,1,3,0:T(8,128)} %get-tuple-element.52, bf16[2048,4,128,1]{0,2,3,1:T(8,128)(2,1)} %bitcast.131, bf16[128,4,8,128]{0,3,2,1:T(8,128)(2,1)S(1)} %bitcast.126, f32[4,8,128]{2,1,0:T(8,128)S(1)} %bitcast.132, f32[4,8,128]{2,1,0:T(8,128)S(1)} %log_add_fusion, ...), kind=kOutput, calls=%fused_computation.3 | convolution fusion | flops 2206203904 | bytes 53772288 | tf_op jit(solution)/shard_map/tghd,sgd->ghts/dot_general | solution.py:94
  233.7 9.8 %fusion.8 = bf16[2048,4,128]{2,0,1:T(8,128)(2,1)} fusion(bf16[4,8,128,2048]{2,3,1,0:T(8,128)(2,1)} %fusion.2, bf16[128,4,8,128]{3,2,1,0:T(8,128)(2,1)S(1)} %bitcast.118), kind=kOutput, calls=%fused_computation.16 | convolution fusion | flops 2148532224 | bytes 19922944 | tf_op jit(solution)/shard_map/ghts,tghd->sgd/dot_general | solution.py:107
  243.5 4.0 %copy.74 = bf16[2048,4,128]{0,2,1:T(8,128)(2,1)} copy(bf16[2048,4,128]{2,0,1:T(8,128)(2,1)} %fusion.8) | data formatting | bytes 4194304 | tf_op jit(solution)/shard_map/convert_element_type | solution.py:109
  247.5 2.2 copy.102
  251.6 5.7 %all-to-all-start.2 = ((bf16[16,128,512]{1,2,0:T(8,128)(2,1)}), bf16[16,128,512]{1,2,0:T(8,128)(2,1)}, u32[]{:S(2)}, u32[]{:S(2)}) async-start(bf16[16,128,512]{1,2,0:T(8,128)(2,1)} %copy.75), calls=%async_computation.2 | async-start | bytes 4194304 | tf_op jit(solution)/shard_map/all_to_all | solution.py:112
  257.3 2.4 copy.84
  259.7 9.2 %convolution_convert_fusion = bf16[4,128,8,128]{3,1,2,0:T(8,128)(2,1)} fusion(bf16[2048,4,128,1]{0,2,3,1:T(8,128)(2,1)S(1)} %bitcast.108, bf16[4,8,128,2048]{2,3,1,0:T(8,128)(2,1)} %fusion.2), kind=kOutput, calls=%fused_computation.19 | convolution fusion | flops 2148007936 | bytes 19922944 | tf_op jit(solution)/shard_map/ghts,sgd->tghd/dot_general | solution.py:102
  268.9 2.3 copy.81
  271.1 2.3 copy.80
  273.4 15.8 %all-to-all-done.2 = bf16[16,128,512]{1,2,0:T(8,128)(2,1)} async-done(((bf16[16,128,512]{1,2,0:T(8,128)(2,1)}), bf16[16,128,512]{1,2,0:T(8,128)(2,1)}, u32[]{:S(2)}, u32[]{:S(2)}) %all-to-all-start.2) | async-done | bytes 2097184 | tf_op jit(solution)/shard_map/all_to_all | solution.py:112
  291.9 4.7 %fusion.7 = bf16[1,128,4096]{2,1,0:T(8,128)(2,1)} fusion(bf16[128,512]{0,1:T(8,128)(2,1)S(1)} %reduce_sum.55, bf16[4096,512]{1,0:T(8,128)(2,1)} %bitcast.110), kind=kOutput, calls=%fused_computation.13 | convolution fusion | flops 537919488 | bytes 5373952 | tf_op jit(solution)/shard_map/dot_general | solution.py:123
  (29 shorter events, 13.4 us)
Async XLA Ops:
  7.2 89.1 %copy-start = (bf16[1,128,4096]{2,1,0:T(8,128)(2,1)S(1)}, bf16[1,128,4096]{2,1,0:T(8,128)(2,1)}, u32[]{:S(2)}) copy-start(bf16[1,128,4096]{2,1,0:T(8,128)(2,1)} %param.8) | copy-start | bytes 3145732
  7.2 78.4 %all-gather.6.cloned.1.call-start = ((), (), s32[]{:S(2)}) async-start(), calls=%async_computation.7 | async-start | bytes 6684672 | tf_op jit(solution)/shard_map/all_gather | solution.py:30
  38.7 16.9 %all-to-all-start.1 = ((bf16[8,256,256]{2,1,0:T(8,128)(2,1)}), bf16[8,256,256]{2,1,0:T(8,128)(2,1)S(1)}, u32[]{:S(2)}, u32[]{:S(2)}) async-start(bf16[8,256,256]{2,1,0:T(8,128)(2,1)} %broadcast_in_dim.37), calls=%async_computation.1 | async-start | bytes 2097152 | tf_op jit(solution)/shard_map/all_to_all | solution.py:49
  42.3 106.1 %all-gather.4.cloned.1.call-start = ((), (), s32[]{:S(2)}) async-start(), calls=%async_computation.5 | async-start | bytes 2228224 | tf_op jit(solution)/shard_map/all_gather | solution.py:62
  100.4 196.1 %reduce-scatter.2.cloned.1.call-start = ((), (), s32[]{:S(2)}) async-start(), calls=%async_computation.6 | async-start | bytes 4456448 | tf_op jit(solution)/shard_map/reduce_scatter | solution.py:120
  193.8 17.5 %copy-start.3 = (bf16[1,128,4096]{1,2,0:T(8,128)(2,1)S(1)}, bf16[1,128,4096]{1,2,0:T(8,128)(2,1)}, u32[]{:S(2)}) copy-start(bf16[1,128,4096]{1,2,0:T(8,128)(2,1)} %copy.67) | copy-start | bytes 3145732
  211.3 22.5 %copy-start.2 = (bf16[16,8,32,128]{3,2,1,0:T(8,128)(2,1)S(1)}, bf16[16,8,32,128]{3,2,1,0:T(8,128)(2,1)}, u32[]{:S(2)}) copy-start(bf16[16,8,32,128]{3,2,1,0:T(8,128)(2,1)} %copy.101) | copy-start | bytes 3145732
  251.6 37.6 %all-to-all-start.2 = ((bf16[16,128,512]{1,2,0:T(8,128)(2,1)}), bf16[16,128,512]{1,2,0:T(8,128)(2,1)}, u32[]{:S(2)}, u32[]{:S(2)}) async-start(bf16[16,128,512]{1,2,0:T(8,128)(2,1)} %copy.75), calls=%async_computation.2 | async-start | bytes 4194304 | tf_op jit(solution)/shard_map/all_to_all | solution.py:112
  257.3 41.2 %copy-start.1 = (bf16[1,128,4096]{2,1,0:T(8,128)(2,1)S(1)}, bf16[1,128,4096]{2,1,0:T(8,128)(2,1)}, u32[]{:S(2)}) copy-start(bf16[1,128,4096]{2,1,0:T(8,128)(2,1)} %param.8) | copy-start | bytes 3145732
Sparse Core Ops, SparseCore 0:
  11.0 74.5 all-gather.5
  100.6 47.7 all-gather.3
  193.9 85.6 reduce-scatter.1
where the time goes:
time: 306 us; the launch traced here: 305 us
  matrix products  102 us (33%)
  blocking collectives  57 us (19%)
  waiting for transfers between devices  55.2 us (18%)
  local copies, waits for them, and re-layouts  44.3 us (14%)
  other arithmetic  23.1 us (8%)
  between operations  13.9 us (5%)
  starting transfers between devices  9.57 us (3%)
    all_to_all x1, blocking collectives, on_device(): lax.all_to_all(value_term.reshape(fsdp_size, tok_rows, kv_width), 'fsdp',...  32.5 us
    all_gather x1, waiting for transfers between devices, on_device(): lax.all_gather(jnp.concatenate([keys, value_weight], axis=0), 'fsdp', axi...  28.6 us
    all_to_all x1, blocking collectives, on_device(): lax.all_to_all(frag_local[0].reshape(frag_rows, replicas, share_cols).tra...  24.6 us
    dot_general x1, matrix products, on_device(): jnp.einsum('tghd,sgd->ghts', grad_heads, value_groups, preferred_element_...  22.5 us
    dot_general x1, matrix products, on_device(): jnp.einsum('ghts,sgd->tghd', probs_low, value_groups, preferred_element_t...  17.5 us
    unnamed x17, local copies, waits for them, and re-layouts  17.1 us
    dot_general x1, matrix products, on_device(): jnp.einsum('ghts,tghd->sgd', probs_low, grad_heads, preferred_element_typ...  16.1 us
    all_to_all x1, waiting for transfers between devices, on_device(): lax.all_to_all(key_term.reshape(fsdp_size, tok_rows, kv_width), 'fsdp', 0...  15.8 us
  transfers between devices with their start and end apart: 5, of which 4 were waited for; matrix products, arithmetic and copies ran while one was open for 45% of the time, Pallas kernels for 0%

commit v1 on v0

--- a/solution.py
+++ b/solution.py
@@ -81,7 +81,6 @@
         .reshape(length_all, kv_heads * HD)
         .astype(jnp.bfloat16)
     )
-    value_term, values_all = lax.optimization_barrier((value_term, values_all))
     kv_width = value_term.shape[1]
     value_parts = lax.all_to_all(
         value_term.reshape(fsdp_size, tok_rows, kv_width), "fsdp", 0, 0, tiled=True
@@ -109,6 +108,7 @@
         .astype(jnp.bfloat16)
     )
     context = context_heads.reshape(tok_rows, queries.shape[1])
+    key_term, token_source = lax.optimization_barrier((key_term, value_grad))
     key_parts = lax.all_to_all(
         key_term.reshape(fsdp_size, tok_rows, kv_width), "fsdp", 0, 0, tiled=True
     )
@@ -121,7 +121,7 @@
         weight_term, "fsdp", scatter_dimension=0, tiled=True
     ).astype(jnp.float32)
     token_sum = lax.dot_general(
-        value_grad,
+        token_source,
         weight_all,
         (((1,), (1,)), ((), ())),
         preferred_element_type=jnp.float32,

time: 306 us -> 288 us (0.941)
  matrix products: 102 us -> 91.6 us
  waiting for transfers between devices: 55.2 us -> 49 us
    dot_general x1, matrix products: 22.5 us -> 17 us  [on_device(): jnp.einsum('tghd,sgd->ghts', grad_heads, value_groups, preferred_element_...]
    all_to_all x1, waiting for transfers between devices: 15.8 us -> 11.8 us  [on_device(): lax.all_to_all(key_term.reshape(fsdp_size, tok_rows, kv_width), 'fsdp', 0...]
    unnamed x17 -> x32, local copies, waits for them, and re-layouts: 17.1 us -> 18.9 us
  transfers between devices with their start and end apart: 5 -> 5, of which waited for: 4 -> 3; matrix products, arithmetic and copies ran while one was open for 45% -> 49% of each run, Pallas kernels for 0% -> 0%
where the time goes in v1:
time: 288 us; the launch traced here: 287 us
  matrix products  91.6 us (32%)
  blocking collectives  55.8 us (19%)
  waiting for transfers between devices  49 us (17%)
  local copies, waits for them, and re-layouts  45.6 us (16%)
  other arithmetic  21.8 us (8%)
  between operations  14 us (5%)
  starting transfers between devices  9.51 us (3%)
    all_to_all x1, blocking collectives, on_device(): lax.all_to_all(value_term.reshape(fsdp_size, tok_rows, kv_width), 'fsdp',...  31.2 us
    all_gather x1, waiting for transfers between devices, on_device(): lax.all_gather(jnp.concatenate([keys, value_weight], axis=0), 'fsdp', axi...  28.5 us
    all_to_all x1, blocking collectives, on_device(): lax.all_to_all(frag_local[0].reshape(frag_rows, replicas, share_cols).tra...  24.6 us
    unnamed x32, local copies, waits for them, and re-layouts  18.9 us
    dot_general x1, matrix products, on_device(): jnp.einsum('ghts,sgd->tghd', probs_low, value_groups, preferred_element_t...  17.8 us
    dot_general x1, matrix products, on_device(): jnp.einsum('tghd,sgd->ghts', grad_heads, value_groups, preferred_element_...  17 us
    dot_general x1, matrix products, on_device(): jnp.einsum('ghts,tghd->sgd', probs_low, grad_heads, preferred_element_typ...  15.6 us
    dot_general x1, matrix products, on_device(): jnp.einsum('tghd,sgd->ghts', query_heads, key_groups, preferred_element_t...  15.3 us
  transfers between devices with their start and end apart: 5, of which 3 were waited for; matrix products, arithmetic and copies ran while one was open for 49% of the time, Pallas kernels for 0%

profile of v1, /device:TPU:1, one launch (start us, length us, event | category | flops | bytes accessed | tf_op | source)
XLA Modules:
  0.0 287.3 jit_solution(16042971027453589741)
XLA Ops:
  7.2 1.8 pad_maximum_fusion
  11.1 24.6 %all_to_all.20 = bf16[8,256,256]{2,1,0:T(8,128)(2,1)S(1)} all-to-all(bf16[8,256,256]{2,1,0:T(8,128)(2,1)S(1)} %copy.65), channel_id=1, replica_groups=mesh['replica'=8,'fsdp'=16] {'replica'}, dimensions={0} | all-to-all | bytes 2097152 | tf_op jit(solution)/shard_map/all_to_all | solution.py:38
  35.8 1.9 fusion.19
  38.8 3.6 %all-to-all-start.1 = ((bf16[8,256,256]{2,1,0:T(8,128)(2,1)}), bf16[8,256,256]{2,1,0:T(8,128)(2,1)S(1)}, u32[]{:S(2)}, u32[]{:S(2)}) async-start(bf16[8,256,256]{2,1,0:T(8,128)(2,1)} %broadcast_in_dim.37), calls=%async_computation.1 | async-start | bytes 2097152 | tf_op jit(solution)/shard_map/all_to_all | solution.py:49
  42.4 2.3 copy.71
  44.7 2.3 copy.106
  47.1 8.7 %all-to-all-done.1 = bf16[8,256,256]{2,1,0:T(8,128)(2,1)S(1)} async-done(((bf16[8,256,256]{2,1,0:T(8,128)(2,1)}), bf16[8,256,256]{2,1,0:T(8,128)(2,1)S(1)}, u32[]{:S(2)}, u32[]{:S(2)}) %all-to-all-start.1) | async-done | bytes 1048608 | tf_op jit(solution)/shard_map/all_to_all | solution.py:49
  57.1 28.5 %all-gather.6.cloned.1.call-done = bf16[6144,512]{1,0:T(8,128)(2,1)} async-done(((bf16[384,512]{1,0:T(8,128)(2,1)}), bf16[6144,512]{1,0:T(8,128)(2,1)}) %all-gather.6.cloned.1.call-update) | async-done | bytes 6291472 | tf_op jit(solution)/shard_map/all_gather | solution.py:30
  85.6 2.6 slice.8
  88.2 4.6 %slice.9 = bf16[16,128,512]{2,1,0:T(8,128)(2,1)} slice(bf16[16,384,512]{2,1,0:T(8,128)(2,1)} %bitcast.118), slice={[0:16], [0:128], [0:512]} | slice | bytes 4194304 | tf_op jit(solution)/shard_map/slice | solution.py:33
  92.8 2.0 fusion.10
  95.1 2.9 %copy.67 = bf16[2048,512]{0,1:T(8,128)(2,1)S(1)} copy(bf16[2048,512]{1,0:T(8,128)(2,1)} %bitcast.113) | data formatting | bytes 4194304 | tf_op jit(solution)/shard_map/optimization_barrier | solution.py:59
  98.0 15.3 %fusion.4 = (f32[4,8,128]{2,1,0:T(8,128)S(1)}, f32[4,2048,128,8]{2,1,3,0:T(8,128)}) fusion(pred[128,2048]{0,1:T(8,128)(4,1)S(1)} %iota_compare_fusion, bf16[2048,4,128,1]{0,2,3,1:T(8,128)(2,1)S(1)} %bitcast.106, bf16[128,4,8,128]{0,3,2,1:T(8,128)(2,1)} %bitcast.110), kind=kOutput, calls=%fused_computation.8 | convolution fusion | flops 2172645376 | bytes 36978688 | tf_op jit(solution)/shard_map/tghd,sgd->ghts/dot_general | solution.py:70
  113.3 14.5 %exponential_reduce_fusion = f32[4,8,128]{2,1,0:T(8,128)S(1)} fusion(f32[4,2048,128,8]{2,1,3,0:T(8,128)} %get-tuple-element.52, f32[4,8,128]{2,1,0:T(8,128)S(1)} %get-tuple-element.51, pred[128,2048]{0,1:T(8,128)(4,1)S(1)} %iota_compare_fusion), kind=kLoop, calls=%fused_computation.6 | loop fusion | flops 33550336 | bytes 33849344 | tf_op jit(solution)/shard_map/reduce_sum | solution.py:75
  127.9 15.6 %fusion.8 = bf16[2048,4,128]{2,0,1:T(8,128)(2,1)} fusion(bf16[128,4,8,128]{0,3,2,1:T(8,128)(2,1)S(1)} %bitcast.124, f32[4,2048,128,8]{2,1,3,0:T(8,128)} %get-tuple-element.52, f32[4,8,128]{2,1,0:T(8,128)S(1)} %log_add_fusion, pred[128,2048]{0,1:T(8,128)(4,1)S(1)} %iota_compare_fusion), kind=kOutput, calls=%fused_computation.16 | convolution fusion | flops 2182086656 | bytes 36978688 | tf_op jit(solution)/shard_map/ghts,tghd->sgd/dot_general | solution.py:80
  143.5 2.9 %copy.78 = bf16[2048,4,128]{0,2,1:T(8,128)(2,1)S(1)} copy(bf16[2048,4,128]{2,0,1:T(8,128)(2,1)} %fusion.8) | data formatting | bytes 4194304 | tf_op jit(solution)/shard_map/convert_element_type | solution.py:82
  147.6 31.2 %all_to_all.21 = bf16[16,128,512]{1,2,0:T(8,128)(2,1)S(1)} all-to-all(bf16[16,128,512]{1,2,0:T(8,128)(2,1)S(1)} %copy.79), channel_id=1, replica_groups=mesh['replica'=8,'fsdp'=16] {'fsdp'}, dimensions={0} | all-to-all | bytes 4194304 | tf_op jit(solution)/shard_map/all_to_all | solution.py:85
  179.1 3.2 %fusion.5 = bf16[4096,512]{0,1:T(8,128)(2,1)} fusion(bf16[128,512]{0,1:T(8,128)(2,1)S(1)} %reduce_sum.54, bf16[1,128,4096]{2,1,0:T(8,128)(2,1)S(1)} %copy-done), kind=kOutput, calls=%fused_computation.10 | convolution fusion | flops 541065216 | bytes 5373952 | tf_op jit(solution)/shard_map/dot_general | solution.py:116
  182.4 17.8 %multiply_reduce_fusion = (f32[128,4,8]{0,2,1:T(8,128)}, bf16[4,128,8,128]{3,1,2,0:T(8,128)(2,1)}) fusion(bf16[128,4,8,128]{0,3,2,1:T(8,128)(2,1)} %bitcast.122, bf16[2048,4,128,1]{0,2,3,1:T(8,128)(2,1)} %bitcast.128, f32[4,2048,128,8]{2,1,3,0:T(8,128)} %get-tuple-element.52, f32[4,8,128]{2,1,0:T(8,128)S(1)} %log_add_fusion, ...), kind=kOutput, calls=%fused_computation.17 | convolution fusion | flops 2183655424 | bytes 38043648 | tf_op jit(solution)/shard_map/ghts,sgd->tghd/dot_general | solution.py:90
  200.2 17.0 %fusion.2 = bf16[4,8,128,2048]{2,3,1,0:T(8,128)(2,1)S(1)} fusion(f32[4,2048,128,8]{2,1,3,0:T(8,128)} %get-tuple-element.52, bf16[2048,4,128,1]{0,2,3,1:T(8,128)(2,1)} %bitcast.129, bf16[128,4,8,128]{0,3,2,1:T(8,128)(2,1)} %bitcast.123, f32[4,8,128]{2,1,0:T(8,128)} %bitcast.130, f32[4,8,128]{2,1,0:T(8,128)} %copy-done.11, pred[128,2048]{0,1:T(8,128)(4,1)} %copy-done.6), kind=kOutput, calls=%fused_computation.3 | convolution fusion | flops 2206203904 | bytes 53772288 | tf_op jit(solution)/shard_map/tghd,sgd->ghts/dot_general | solution.py:93
  217.2 5.7 %copy-done.2 = bf16[4,8,128,2048]{2,3,1,0:T(8,128)(2,1)} copy-done((bf16[4,8,128,2048]{2,3,1,0:T(8,128)(2,1)}, bf16[4,8,128,2048]{2,3,1,0:T(8,128)(2,1)S(1)}, u32[]{:S(2)}) %copy-start.2) | copy-done | bytes 16777240
  222.9 6.9 %bitcast_convert_fusion.1 = bf16[4,2048,128]{1,2,0:T(8,128)(2,1)} fusion(bf16[4,8,128,2048]{2,3,1,0:T(8,128)(2,1)S(1)} %fusion.2, bf16[128,4,8,128]{0,3,2,1:T(8,128)(2,1)S(1)} %bitcast.111), kind=kOutput, calls=%fused_computation.15 | convolution fusion | flops 2148532224 | bytes 19922944 | tf_op jit(solution)/shard_map/ghts,tghd->sgd/dot_general | solution.py:106
  229.8 4.1 %copy.81 = bf16[2048,512]{1,0:T(8,128)(2,1)} copy(bf16[2048,512]{0,1:T(8,128)(2,1)} %bitcast.112) | data formatting | bytes 4194304 | tf_op jit(solution)/shard_map/optimization_barrier | solution.py:111
  233.9 3.9 %copy.82 = bf16[16,128,512]{1,2,0:T(8,128)(2,1)} copy(bf16[16,128,512]{2,1,0:T(8,128)(2,1)} %bitcast.116) | data formatting | bytes 4194304 | tf_op jit(solution)/shard_map/reshape | solution.py:113
  237.9 5.6 %all-to-all-start.3 = ((bf16[16,128,512]{1,2,0:T(8,128)(2,1)}), bf16[16,128,512]{1,2,0:T(8,128)(2,1)}, u32[]{:S(2)}, u32[]{:S(2)}) async-start(bf16[16,128,512]{1,2,0:T(8,128)(2,1)} %copy.82), calls=%async_computation.3 | async-start | bytes 4194304 | tf_op jit(solution)/shard_map/all_to_all | solution.py:112
  243.5 2.3 copy.88
  245.8 2.4 copy.84
  248.2 9.2 %convolution_convert_fusion = bf16[4,128,8,128]{3,1,2,0:T(8,128)(2,1)} fusion(bf16[2048,4,128,1]{0,2,3,1:T(8,128)(2,1)S(1)} %bitcast.107, bf16[4,8,128,2048]{2,3,1,0:T(8,128)(2,1)} %copy-done.2), kind=kOutput, calls=%fused_computation.19 | convolution fusion | flops 2148007936 | bytes 19922944 | tf_op jit(solution)/shard_map/ghts,sgd->tghd/dot_general | solution.py:101
  257.4 2.3 copy.85
  259.6 4.7 %fusion.7 = bf16[1,128,4096]{2,1,0:T(8,128)(2,1)} fusion(bf16[128,512]{0,1:T(8,128)(2,1)S(1)} %copy-done.9, bf16[4096,512]{1,0:T(8,128)(2,1)} %bitcast.109), kind=kOutput, calls=%fused_computation.13 | convolution fusion | flops 537919488 | bytes 5373952 | tf_op jit(solution)/shard_map/dot_general | solution.py:123
  264.3 11.8 %all-to-all-done.3 = bf16[16,128,512]{1,2,0:T(8,128)(2,1)} async-done(((bf16[16,128,512]{1,2,0:T(8,128)(2,1)}), bf16[16,128,512]{1,2,0:T(8,128)(2,1)}, u32[]{:S(2)}, u32[]{:S(2)}) %all-to-all-start.3) | async-done | bytes 2097184 | tf_op jit(solution)/shard_map/all_to_all | solution.py:112
  276.1 1.9 reduce_sum.55
  (45 shorter events, 9.3 us)
Async XLA Ops:
  7.2 85.7 %copy-start = (bf16[1,128,4096]{2,1,0:T(8,128)(2,1)S(1)}, bf16[1,128,4096]{2,1,0:T(8,128)(2,1)}, u32[]{:S(2)}) copy-start(bf16[1,128,4096]{2,1,0:T(8,128)(2,1)} %param.8) | copy-start | bytes 3145732
  7.2 78.4 %all-gather.6.cloned.1.call-start = ((), (), s32[]{:S(2)}) async-start(), calls=%async_computation.7 | async-start | bytes 6684672 | tf_op jit(solution)/shard_map/all_gather | solution.py:30
  38.8 17.0 %all-to-all-start.1 = ((bf16[8,256,256]{2,1,0:T(8,128)(2,1)}), bf16[8,256,256]{2,1,0:T(8,128)(2,1)S(1)}, u32[]{:S(2)}, u32[]{:S(2)}) async-start(bf16[8,256,256]{2,1,0:T(8,128)(2,1)} %broadcast_in_dim.37), calls=%async_computation.1 | async-start | bytes 2097152 | tf_op jit(solution)/shard_map/all_to_all | solution.py:49
  42.3 140.0 %all-gather.4.cloned.1.call-start = ((), (), s32[]{:S(2)}) async-start(), calls=%async_computation.5 | async-start | bytes 2228224 | tf_op jit(solution)/shard_map/all_gather | solution.py:62
  47.1 135.2 %copy-start.6 = (pred[128,2048]{0,1:T(8,128)(4,1)}, pred[128,2048]{0,1:T(8,128)(4,1)S(1)}, u32[]{:S(2)}) copy-start(pred[128,2048]{0,1:T(8,128)(4,1)S(1)} %iota_compare_fusion) | copy-start | bytes 786436
  88.2 4.6 %copy-start.5 = (bf16[16,256,512]{2,1,0:T(8,128)(2,1)}, bf16[16,256,512]{2,1,0:T(8,128)(2,1)S(1)}, u32[]{:S(2)}) copy-start(bf16[16,256,512]{2,1,0:T(8,128)(2,1)S(1)} %slice.8) | copy-start | bytes 12582916
  94.8 183.9 %reduce-scatter.2.cloned.1.call-start = ((), (), s32[]{:S(2)}) async-start(), calls=%async_computation.6 | async-start | bytes 4456448 | tf_op jit(solution)/shard_map/reduce_scatter | solution.py:120
  98.0 15.3 %copy-start.3 = (bf16[2048,512]{0,1:T(8,128)(2,1)}, bf16[2048,512]{0,1:T(8,128)(2,1)S(1)}, u32[]{:S(2)}) copy-start(bf16[2048,512]{0,1:T(8,128)(2,1)S(1)} %copy.67) | copy-start | bytes 6291460
  113.3 14.6 %copy-start.10 = (bf16[1,128,4096]{1,2,0:T(8,128)(2,1)S(1)}, bf16[1,128,4096]{1,2,0:T(8,128)(2,1)}, u32[]{:S(2)}) copy-start(bf16[1,128,4096]{1,2,0:T(8,128)(2,1)} %copy.71) | copy-start | bytes 3145732
  127.9 54.5 %copy-start.11 = (f32[4,8,128]{2,1,0:T(8,128)}, f32[4,8,128]{2,1,0:T(8,128)S(1)}, u32[]{:S(2)}) copy-start(f32[4,8,128]{2,1,0:T(8,128)S(1)} %log_add_fusion) | copy-start | bytes 49156
  179.1 21.1 %copy-start.8 = (bf16[128,512]{0,1:T(8,128)(2,1)}, bf16[128,512]{0,1:T(8,128)(2,1)S(1)}, u32[]{:S(2)}) copy-start(bf16[128,512]{0,1:T(8,128)(2,1)S(1)} %reduce_sum.54) | copy-start | bytes 393220
  200.2 22.7 %copy-start.7 = (bf16[1,128,4096]{1,2,0:T(8,128)(2,1)S(1)}, bf16[1,128,4096]{1,2,0:T(8,128)(2,1)}, u32[]{:S(2)}) copy-start(bf16[1,128,4096]{1,2,0:T(8,128)(2,1)} %copy.106) | copy-start | bytes 3145732
  217.2 5.7 %copy-start.2 = (bf16[4,8,128,2048]{2,3,1,0:T(8,128)(2,1)}, bf16[4,8,128,2048]{2,3,1,0:T(8,128)(2,1)S(1)}, u32[]{:S(2)}) copy-start(bf16[4,8,128,2048]{2,3,1,0:T(8,128)(2,1)S(1)} %fusion.2) | copy-start | bytes 50331652
  229.8 18.4 %copy-start.4 = (bf16[2048,512]{0,1:T(8,128)(2,1)S(1)}, bf16[2048,512]{0,1:T(8,128)(2,1)}, u32[]{:S(2)}) copy-start(bf16[2048,512]{0,1:T(8,128)(2,1)} %copy-done.3) | copy-start | bytes 6291460
  233.9 25.7 %copy-start.9 = (bf16[128,512]{0,1:T(8,128)(2,1)S(1)}, bf16[128,512]{0,1:T(8,128)(2,1)}, u32[]{:S(2)}) copy-start(bf16[128,512]{0,1:T(8,128)(2,1)} %copy-done.8) | copy-start | bytes 393220
  237.9 38.2 %all-to-all-start.3 = ((bf16[16,128,512]{1,2,0:T(8,128)(2,1)}), bf16[16,128,512]{1,2,0:T(8,128)(2,1)}, u32[]{:S(2)}, u32[]{:S(2)}) async-start(bf16[16,128,512]{1,2,0:T(8,128)(2,1)} %copy.82), calls=%async_computation.3 | async-start | bytes 4194304 | tf_op jit(solution)/shard_map/all_to_all | solution.py:112
  245.8 35.0 %copy-start.1 = (bf16[1,128,4096]{2,1,0:T(8,128)(2,1)S(1)}, bf16[1,128,4096]{2,1,0:T(8,128)(2,1)}, u32[]{:S(2)}) copy-start(bf16[1,128,4096]{2,1,0:T(8,128)(2,1)} %param.8) | copy-start | bytes 3145732
Sparse Core Ops, SparseCore 0:
  11.0 74.5 all-gather.5
  94.9 47.7 all-gather.3
  182.4 94.8 reduce-scatter.1

commit v2 on v1

--- a/solution.py
+++ b/solution.py
@@ -32,31 +32,6 @@
     )
     keys_all = gathered[:, :key_rows].reshape(fsdp_size * key_rows, keys.shape[1])
     weight_all = gathered[:, key_rows:].reshape(fsdp_size * weight_rows, value_weight.shape[1])
-    replicas = lax.axis_size("replica")
-    share_cols = frag_global.shape[1]
-    frag_rows = frag_global.shape[0]
-    local_parts = lax.all_to_all(
-        frag_local[0].reshape(frag_rows, replicas, share_cols).transpose(1, 0, 2),
-        "replica",
-        0,
-        0,
-        tiled=True,
-    )
-    own_sum = jnp.sum(local_parts.astype(jnp.float32), axis=0)
-    delta = frag_global - own_sum / replicas
-    new_momentum = outer_momentum * frag_momentum + delta
-    new_global = frag_global - outer_rate * (delta + outer_momentum * new_momentum)
-    refreshed_parts = lax.all_to_all(
-        jnp.broadcast_to(
-            new_global.astype(jnp.bfloat16)[None], (replicas, frag_rows, share_cols)
-        ),
-        "replica",
-        0,
-        0,
-        tiled=True,
-    )
-    refreshed_local = refreshed_parts.transpose(1, 0, 2).reshape(frag_rows, replicas * share_cols)
-    refreshed_local, keys_all = lax.optimization_barrier((refreshed_local, keys_all))
     value_sum = jnp.dot(tokens, weight_all, preferred_element_type=jnp.float32)
     values = (value_sum * proj_scale).astype(jnp.bfloat16)
     values_all = lax.all_gather(values, "fsdp", axis=0, tiled=True)
@@ -86,6 +61,31 @@
         value_term.reshape(fsdp_size, tok_rows, kv_width), "fsdp", 0, 0, tiled=True
     )
     value_grad = jnp.sum(value_parts.astype(jnp.float32), axis=0).astype(jnp.bfloat16)
+    late_local, value_grad = lax.optimization_barrier((frag_local, value_grad))
+    replicas = lax.axis_size("replica")
+    share_cols = frag_global.shape[1]
+    frag_rows = frag_global.shape[0]
+    local_parts = lax.all_to_all(
+        late_local[0].reshape(frag_rows, replicas, share_cols).transpose(1, 0, 2),
+        "replica",
+        0,
+        0,
+        tiled=True,
+    )
+    own_sum = jnp.sum(local_parts.astype(jnp.float32), axis=0)
+    delta = frag_global - own_sum / replicas
+    new_momentum = outer_momentum * frag_momentum + delta
+    new_global = frag_global - outer_rate * (delta + outer_momentum * new_momentum)
+    refreshed_parts = lax.all_to_all(
+        jnp.broadcast_to(
+            new_global.astype(jnp.bfloat16)[None], (replicas, frag_rows, share_cols)
+        ),
+        "replica",
+        0,
+        0,
+        tiled=True,
+    )
+    refreshed_local = refreshed_parts.transpose(1, 0, 2).reshape(frag_rows, replicas * share_cols)
     value_groups = values_all.reshape(length_all, kv_heads, HD)
     context_heads = jnp.einsum(
         "ghts,sgd->tghd", probs_low, value_groups, preferred_element_type=jnp.float32

time: 288 us -> 304 us (1.056)
  waiting for transfers between devices: 49 us -> 79.8 us
  blocking collectives: 55.8 us -> 31.4 us
  starting transfers between devices: 9.51 us -> 16.1 us
  local copies, waits for them, and re-layouts: 45.6 us -> 49 us
    all_gather x1, waiting for transfers between devices: 28.5 us -> 64.6 us  [on_device(): lax.all_gather(jnp.concatenate([keys, value_weight], axis=0), 'fsdp', axi...]
    all_to_all x1 -> x0, blocking collectives: 24.6 us -> none  [on_device(): lax.all_to_all(frag_local[0].reshape(frag_rows, replicas, share_cols).tra...]
    all_to_all x0 -> x1, waiting for transfers between devices: none -> 10.8 us  [on_device(): lax.all_to_all(late_local[0].reshape(frag_rows, replicas, share_cols).tra...]
    all_to_all x1, waiting for transfers between devices: 8.67 us -> 0.01 us  [on_device(): lax.all_to_all(jnp.broadcast_to(new_global.astype(jnp.bfloat16)[None], (r...]
    all_to_all x1, waiting for transfers between devices: 11.8 us -> 4.38 us  [on_device(): lax.all_to_all(key_term.reshape(fsdp_size, tok_rows, kv_width), 'fsdp', 0...]
    another operation x0 -> x2, local copies, waits for them, and re-layouts: none -> 5.55 us  [on_device(): key_groups = keys_all.reshape(length_all, kv_heads, HD)]
    all_to_all x0 -> x1, starting transfers between devices: none -> 4.92 us  [on_device(): lax.all_to_all(late_local[0].reshape(frag_rows, replicas, share_cols).tra...]
  transfers between devices with their start and end apart: 5 -> 6, of which waited for: 3 -> 3; matrix products, arithmetic and copies ran while one was open for 49% -> 47% of each run, Pallas kernels for 0% -> 0%
where the time goes in v2:
time: 304 us; the launch traced here: 303 us
  matrix products  90.3 us (30%)
  waiting for transfers between devices  79.8 us (26%)
  local copies, waits for them, and re-layouts  49 us (16%)
  blocking collectives  31.4 us (10%)
  other arithmetic  21.8 us (7%)
  starting transfers between devices  16.1 us (5%)
  between operations  14 us (5%)
    all_gather x1, waiting for transfers between devices, on_device(): lax.all_gather(jnp.concatenate([keys, value_weight], axis=0), 'fsdp', axi...  64.6 us
    all_to_all x1, blocking collectives, on_device(): lax.all_to_all(value_term.reshape(fsdp_size, tok_rows, kv_width), 'fsdp',...  31.4 us
    unnamed x32, local copies, waits for them, and re-layouts  19.9 us
    dot_general x1, matrix products, on_device(): jnp.einsum('ghts,sgd->tghd', probs_low, value_groups, preferred_element_t...  17.4 us
    dot_general x1, matrix products, on_device(): jnp.einsum('tghd,sgd->ghts', grad_heads, value_groups, preferred_element_...  16.6 us
    dot_general x1, matrix products, on_device(): jnp.einsum('ghts,tghd->sgd', probs_low, grad_heads, preferred_element_typ...  15.7 us
    dot_general x1, matrix products, on_device(): jnp.einsum('tghd,sgd->ghts', query_heads, key_groups, preferred_element_t...  14.9 us
    reduce_sum x1, other arithmetic, on_device(): summed = jnp.sum(jnp.exp(scores - top), axis=-1, keepdims=True)  14.6 us
  transfers between devices with their start and end apart: 6, of which 3 were waited for; matrix products, arithmetic and copies ran while one was open for 47% of the time, Pallas kernels for 0%

profile of v2, /device:TPU:1, one launch (start us, length us, event | category | flops | bytes accessed | tf_op | source)
XLA Modules:
  0.0 302.5 jit_solution(12700232333470374015)
XLA Ops:
  9.1 2.3 copy.67
  11.4 2.3 copy.106
  13.9 64.6 %all-gather.6.cloned.1.call-done = bf16[6144,512]{1,0:T(8,128)(2,1)} async-done(((bf16[384,512]{1,0:T(8,128)(2,1)}), bf16[6144,512]{1,0:T(8,128)(2,1)}) %all-gather.6.cloned.1.call-update) | async-done | bytes 6291472 | tf_op jit(solution)/shard_map/all_gather | solution.py:30
  78.4 2.6 slice.8
  81.0 4.6 %slice.9 = bf16[16,128,512]{2,1,0:T(8,128)(2,1)} slice(bf16[16,384,512]{2,1,0:T(8,128)(2,1)} %bitcast.120), slice={[0:16], [0:128], [0:512]} | slice | bytes 4194304 | tf_op jit(solution)/shard_map/slice | solution.py:33
  85.6 2.0 fusion.17
  87.6 3.4 %copy.105 = bf16[16,128,512]{1,0,2:T(8,128)(2,1)S(1)} copy(bf16[16,128,512]{2,1,0:T(8,128)(2,1)} %slice.9) | data formatting | bytes 4194304
  91.1 2.7 reshape_reshape.3
  93.8 14.9 %fusion.4 = (f32[4,8,128]{2,1,0:T(8,128)S(1)}, f32[4,2048,128,8]{2,1,3,0:T(8,128)}) fusion(pred[128,2048]{0,1:T(8,128)(4,1)S(1)} %iota_compare_fusion, bf16[128,4,8,128]{0,3,2,1:T(8,128)(2,1)} %bitcast.113, bf16[2048,4,128]{0,2,1:T(8,128)(2,1)} %reshape_reshape.3), kind=kOutput, calls=%fused_computation.8 | convolution fusion | flops 2172645376 | bytes 36978688 | tf_op jit(solution)/shard_map/tghd,sgd->ghts/dot_general | solution.py:45
  108.6 14.6 %exponential_reduce_fusion = f32[4,8,128]{2,1,0:T(8,128)S(1)} fusion(f32[4,2048,128,8]{2,1,3,0:T(8,128)} %get-tuple-element.52, f32[4,8,128]{2,1,0:T(8,128)S(1)} %get-tuple-element.51, pred[128,2048]{0,1:T(8,128)(4,1)S(1)} %iota_compare_fusion), kind=kLoop, calls=%fused_computation.6 | loop fusion | flops 33550336 | bytes 33849344 | tf_op jit(solution)/shard_map/reduce_sum | solution.py:50
  123.3 15.7 %fusion.8 = bf16[2048,4,128]{2,0,1:T(8,128)(2,1)} fusion(bf16[128,4,8,128]{0,3,2,1:T(8,128)(2,1)S(1)} %bitcast.125, f32[4,2048,128,8]{2,1,3,0:T(8,128)} %get-tuple-element.52, f32[4,8,128]{2,1,0:T(8,128)S(1)} %log_add_fusion, pred[128,2048]{0,1:T(8,128)(4,1)S(1)} %iota_compare_fusion), kind=kOutput, calls=%fused_computation.16 | convolution fusion | flops 2182086656 | bytes 36978688 | tf_op jit(solution)/shard_map/ghts,tghd->sgd/dot_general | solution.py:55
  138.9 2.9 copy.74
  143.0 31.4 %all_to_all.20 = bf16[16,128,512]{1,2,0:T(8,128)(2,1)S(1)} all-to-all(bf16[16,128,512]{1,2,0:T(8,128)(2,1)S(1)} %copy.75), channel_id=1, replica_groups=mesh['replica'=8,'fsdp'=16] {'fsdp'}, dimensions={0} | all-to-all | bytes 4194304 | tf_op jit(solution)/shard_map/all_to_all | solution.py:60
  177.7 4.9 %all-to-all-start.2 = ((bf16[8,256,256]{2,1,0:T(8,128)(2,1)}), bf16[8,256,256]{2,1,0:T(8,128)(2,1)S(1)}, u32[]{:S(2)}, u32[]{:S(2)}) async-start(bf16[8,256,256]{2,1,0:T(8,128)(2,1)} %copy.81), calls=%async_computation.3 | async-start | bytes 2097152 | tf_op jit(solution)/shard_map/all_to_all | solution.py:68
  182.7 3.2 %fusion.5 = bf16[4096,512]{0,1:T(8,128)(2,1)} fusion(bf16[128,512]{0,1:T(8,128)(2,1)S(1)} %reduce_sum.53, bf16[1,128,4096]{2,1,0:T(8,128)(2,1)S(1)} %copy-done), kind=kOutput, calls=%fused_computation.10 | convolution fusion | flops 541065216 | bytes 5373952 | tf_op jit(solution)/shard_map/dot_general | solution.py:116
  185.9 10.8 %all-to-all-done.2 = bf16[8,256,256]{2,1,0:T(8,128)(2,1)S(1)} async-done(((bf16[8,256,256]{2,1,0:T(8,128)(2,1)}), bf16[8,256,256]{2,1,0:T(8,128)(2,1)S(1)}, u32[]{:S(2)}, u32[]{:S(2)}) %all-to-all-start.2) | async-done | bytes 1048608 | tf_op jit(solution)/shard_map/all_to_all | solution.py:68
  196.8 1.9 fusion.26
  199.8 4.2 %all-to-all-start.3 = ((bf16[8,256,256]{2,1,0:T(8,128)(2,1)}), bf16[8,256,256]{2,1,0:T(8,128)(2,1)}, u32[]{:S(2)}, u32[]{:S(2)}) async-start(bf16[8,256,256]{2,1,0:T(8,128)(2,1)} %broadcast_in_dim.42), calls=%async_computation.4 | async-start | bytes 2097152 | tf_op jit(solution)/shard_map/all_to_all | solution.py:79
  204.1 17.4 %multiply_reduce_fusion = (f32[128,4,8]{0,2,1:T(8,128)}, bf16[4,128,8,128]{3,1,2,0:T(8,128)(2,1)}) fusion(bf16[128,4,8,128]{0,3,2,1:T(8,128)(2,1)S(1)} %bitcast.126, bf16[2048,4,128,1]{0,2,3,1:T(8,128)(2,1)} %bitcast.130, f32[4,2048,128,8]{2,1,3,0:T(8,128)} %get-tuple-element.52, f32[4,8,128]{2,1,0:T(8,128)S(1)} %log_add_fusion, ...), kind=kOutput, calls=%fused_computation.22 | convolution fusion | flops 2183655424 | bytes 38043648 | tf_op jit(solution)/shard_map/ghts,sgd->tghd/dot_general | solution.py:90
  221.5 16.6 %fusion.2 = bf16[4,8,128,2048]{2,3,1,0:T(8,128)(2,1)S(1)} fusion(f32[4,2048,128,8]{2,1,3,0:T(8,128)} %get-tuple-element.52, bf16[2048,4,128,1]{0,2,3,1:T(8,128)(2,1)} %bitcast.131, bf16[128,4,8,128]{0,3,2,1:T(8,128)(2,1)} %bitcast.124, f32[4,8,128]{2,1,0:T(8,128)} %bitcast.132, f32[4,8,128]{2,1,0:T(8,128)} %copy-done.11, pred[128,2048]{0,1:T(8,128)(4,1)} %copy-done.5), kind=kOutput, calls=%fused_computation.3 | convolution fusion | flops 2206203904 | bytes 53772288 | tf_op jit(solution)/shard_map/tghd,sgd->ghts/dot_general | solution.py:93
  238.1 5.7 %copy-done.2 = bf16[4,8,128,2048]{2,3,1,0:T(8,128)(2,1)} copy-done((bf16[4,8,128,2048]{2,3,1,0:T(8,128)(2,1)}, bf16[4,8,128,2048]{2,3,1,0:T(8,128)(2,1)S(1)}, u32[]{:S(2)}) %copy-start.2) | copy-done | bytes 16777240
  243.8 6.8 %bitcast_convert_fusion.1 = bf16[4,2048,128]{1,2,0:T(8,128)(2,1)} fusion(bf16[4,8,128,2048]{2,3,1,0:T(8,128)(2,1)S(1)} %fusion.2, bf16[128,4,8,128]{0,3,2,1:T(8,128)(2,1)S(1)} %bitcast.114), kind=kOutput, calls=%fused_computation.15 | convolution fusion | flops 2148532224 | bytes 19922944 | tf_op jit(solution)/shard_map/ghts,tghd->sgd/dot_general | solution.py:106
  250.7 2.9 copy.77
  253.6 2.4 copy.78
  255.9 6.8 %all-to-all-start.1 = ((bf16[16,128,512]{1,2,0:T(8,128)(2,1)}), bf16[16,128,512]{1,2,0:T(8,128)(2,1)}, u32[]{:S(2)}, u32[]{:S(2)}) async-start(bf16[16,128,512]{1,2,0:T(8,128)(2,1)} %copy.78), calls=%async_computation.1 | async-start | bytes 4194304 | tf_op jit(solution)/shard_map/all_to_all | solution.py:112
  262.8 2.9 reshape.77
  268.6 2.4 copy.83
  270.9 9.1 %fusion.13 = bf16[4,128,8,128]{3,1,2,0:T(8,128)(2,1)} fusion(bf16[4,8,128,2048]{2,3,1,0:T(8,128)(2,1)} %copy-done.2, bf16[2048,4,128,1]{0,2,1,3:T(8,128)(2,1)S(1)} %reshape.77), kind=kOutput, calls=%fused_computation.23 | convolution fusion | flops 2148007936 | bytes 19922944 | tf_op jit(solution)/shard_map/ghts,sgd->tghd/dot_general | solution.py:101
  280.1 2.3 copy.84
  282.3 4.7 %fusion.7 = bf16[1,128,4096]{2,1,0:T(8,128)(2,1)} fusion(bf16[128,512]{0,1:T(8,128)(2,1)S(1)} %copy-done.8, bf16[4096,512]{1,0:T(8,128)(2,1)} %bitcast.112), kind=kOutput, calls=%fused_computation.13 | convolution fusion | flops 537919488 | bytes 5373952 | tf_op jit(solution)/shard_map/dot_general | solution.py:123
  287.0 4.4 %all-to-all-done.1 = bf16[16,128,512]{1,2,0:T(8,128)(2,1)} async-done(((bf16[16,128,512]{1,2,0:T(8,128)(2,1)}), bf16[16,128,512]{1,2,0:T(8,128)(2,1)}, u32[]{:S(2)}, u32[]{:S(2)}) %all-to-all-start.1) | async-done | bytes 2097184 | tf_op jit(solution)/shard_map/all_to_all | solution.py:112
  291.4 1.9 reduce_sum.54
  (48 shorter events, 13.4 us)
Async XLA Ops:
  7.2 78.5 %copy-start = (bf16[1,128,4096]{2,1,0:T(8,128)(2,1)S(1)}, bf16[1,128,4096]{2,1,0:T(8,128)(2,1)}, u32[]{:S(2)}) copy-start(bf16[1,128,4096]{2,1,0:T(8,128)(2,1)} %param.8) | copy-start | bytes 3145732
  7.2 71.2 %all-gather.6.cloned.1.call-start = ((), (), s32[]{:S(2)}) async-start(), calls=%async_computation.7 | async-start | bytes 6684672 | tf_op jit(solution)/shard_map/all_gather | solution.py:30
  9.1 195.0 %all-gather.4.cloned.1.call-start = ((), (), s32[]{:S(2)}) async-start(), calls=%async_computation.5 | async-start | bytes 2228224 | tf_op jit(solution)/shard_map/all_gather | solution.py:37
  13.8 190.2 %copy-start.5 = (pred[128,2048]{0,1:T(8,128)(4,1)}, pred[128,2048]{0,1:T(8,128)(4,1)S(1)}, u32[]{:S(2)}) copy-start(pred[128,2048]{0,1:T(8,128)(4,1)S(1)} %iota_compare_fusion) | copy-start | bytes 786436
  81.0 4.6 %copy-start.4 = (bf16[16,256,512]{2,1,0:T(8,128)(2,1)}, bf16[16,256,512]{2,1,0:T(8,128)(2,1)S(1)}, u32[]{:S(2)}) copy-start(bf16[16,256,512]{2,1,0:T(8,128)(2,1)S(1)} %slice.8) | copy-start | bytes 12582916
  91.1 17.6 %copy-start.3 = (bf16[16,128,512]{1,0,2:T(8,128)(2,1)}, bf16[16,128,512]{1,0,2:T(8,128)(2,1)S(1)}, u32[]{:S(2)}) copy-start(bf16[16,128,512]{1,0,2:T(8,128)(2,1)S(1)} %copy.105) | copy-start | bytes 6291460
  108.6 14.6 %copy-start.9 = (bf16[1,128,4096]{1,2,0:T(8,128)(2,1)S(1)}, bf16[1,128,4096]{1,2,0:T(8,128)(2,1)}, u32[]{:S(2)}) copy-start(bf16[1,128,4096]{1,2,0:T(8,128)(2,1)} %copy.67) | copy-start | bytes 3145732
  123.2 80.8 %copy-start.11 = (f32[4,8,128]{2,1,0:T(8,128)}, f32[4,8,128]{2,1,0:T(8,128)S(1)}, u32[]{:S(2)}) copy-start(f32[4,8,128]{2,1,0:T(8,128)S(1)} %log_add_fusion) | copy-start | bytes 49156
  174.8 46.8 %copy-start.7 = (bf16[128,512]{0,1:T(8,128)(2,1)}, bf16[128,512]{0,1:T(8,128)(2,1)S(1)}, u32[]{:S(2)}) copy-start(bf16[128,512]{0,1:T(8,128)(2,1)S(1)} %reduce_sum.53) | copy-start | bytes 393220
  174.8 29.3 %copy-start.10 = (bf16[1,128,4096]{1,2,0:T(8,128)(2,1)S(1)}, bf16[1,128,4096]{1,2,0:T(8,128)(2,1)}, u32[]{:S(2)}) copy-start(bf16[1,128,4096]{1,2,0:T(8,128)(2,1)} %copy.67) | copy-start | bytes 3145732
  177.7 19.0 %all-to-all-start.2 = ((bf16[8,256,256]{2,1,0:T(8,128)(2,1)}), bf16[8,256,256]{2,1,0:T(8,128)(2,1)S(1)}, u32[]{:S(2)}, u32[]{:S(2)}) async-start(bf16[8,256,256]{2,1,0:T(8,128)(2,1)} %copy.81), calls=%async_computation.3 | async-start | bytes 2097152 | tf_op jit(solution)/shard_map/all_to_all | solution.py:68
  182.6 111.4 %reduce-scatter.2.cloned.1.call-start = ((), (), s32[]{:S(2)}) async-start(), calls=%async_computation.6 | async-start | bytes 4456448 | tf_op jit(solution)/shard_map/reduce_scatter | solution.py:120
  199.8 56.2 %all-to-all-start.3 = ((bf16[8,256,256]{2,1,0:T(8,128)(2,1)}), bf16[8,256,256]{2,1,0:T(8,128)(2,1)}, u32[]{:S(2)}, u32[]{:S(2)}) async-start(bf16[8,256,256]{2,1,0:T(8,128)(2,1)} %broadcast_in_dim.42), calls=%async_computation.4 | async-start | bytes 2097152 | tf_op jit(solution)/shard_map/all_to_all | solution.py:79
  221.5 22.3 %copy-start.6 = (bf16[1,128,4096]{1,2,0:T(8,128)(2,1)S(1)}, bf16[1,128,4096]{1,2,0:T(8,128)(2,1)}, u32[]{:S(2)}) copy-start(bf16[1,128,4096]{1,2,0:T(8,128)(2,1)} %copy.106) | copy-start | bytes 3145732
  238.1 5.7 %copy-start.2 = (bf16[4,8,128,2048]{2,3,1,0:T(8,128)(2,1)}, bf16[4,8,128,2048]{2,3,1,0:T(8,128)(2,1)S(1)}, u32[]{:S(2)}) copy-start(bf16[4,8,128,2048]{2,3,1,0:T(8,128)(2,1)S(1)} %fusion.2) | copy-start | bytes 50331652
  255.9 35.4 %all-to-all-start.1 = ((bf16[16,128,512]{1,2,0:T(8,128)(2,1)}), bf16[16,128,512]{1,2,0:T(8,128)(2,1)}, u32[]{:S(2)}, u32[]{:S(2)}) async-start(bf16[16,128,512]{1,2,0:T(8,128)(2,1)} %copy.78), calls=%async_computation.1 | async-start | bytes 4194304 | tf_op jit(solution)/shard_map/all_to_all | solution.py:112
  262.8 19.6 %copy-start.8 = (bf16[128,512]{0,1:T(8,128)(2,1)S(1)}, bf16[128,512]{0,1:T(8,128)(2,1)}, u32[]{:S(2)}) copy-start(bf16[128,512]{0,1:T(8,128)(2,1)} %copy-done.7) | copy-start | bytes 393220
  268.6 27.5 %copy-start.1 = (bf16[1,128,4096]{2,1,0:T(8,128)(2,1)S(1)}, bf16[1,128,4096]{2,1,0:T(8,128)(2,1)}, u32[]{:S(2)}) copy-start(bf16[1,128,4096]{2,1,0:T(8,128)(2,1)} %param.8) | copy-start | bytes 3145732
Sparse Core Ops, SparseCore 0:
  11.0 67.3 all-gather.5
  87.7 48.0 all-gather.3
  187.5 77.8 reduce-scatter.1

commit v3 on v1

--- a/solution.py
+++ b/solution.py
@@ -117,9 +117,19 @@
         tokens, value_grad, (((0,), (0,)), ((), ())), preferred_element_type=jnp.float32
     )
     weight_term = (product * proj_scale).astype(jnp.bfloat16)
-    weight_grad = lax.psum_scatter(
-        weight_term, "fsdp", scatter_dimension=0, tiled=True
+    split_cols = weight_term.shape[1] // 2
+    weight_left = lax.psum_scatter(
+        weight_term[:, :split_cols], "fsdp", scatter_dimension=0, tiled=True
     ).astype(jnp.float32)
+    weight_parts = lax.all_to_all(
+        weight_term[:, split_cols:].reshape(fsdp_size, weight_rows, split_cols),
+        "fsdp",
+        0,
+        0,
+        tiled=True,
+    )
+    weight_right = jnp.sum(weight_parts.astype(jnp.float32), axis=0)
+    weight_grad = jnp.concatenate([weight_left, weight_right], axis=1)
     token_sum = lax.dot_general(
         token_source,
         weight_all,

time: 288 us -> 287 us (level)
  starting transfers between devices: 9.51 us -> 16.6 us
  local copies, waits for them, and re-layouts: 45.6 us -> 41.3 us
  waiting for transfers between devices: 49 us -> 45.7 us
  matrix products: 91.6 us -> 88.6 us
    all_to_all x1, waiting for transfers between devices: 11.8 us -> 0.89 us  [on_device(): lax.all_to_all(key_term.reshape(fsdp_size, tok_rows, kv_width), 'fsdp', 0...]
    unnamed x32 -> x40, local copies, waits for them, and re-layouts: 18.9 us -> 11.2 us
    reduce_scatter x1, waiting for transfers between devices: 0.01 us -> 5.95 us  [on_device(): lax.psum_scatter(weight_term[:, :split_cols], 'fsdp', scatter_dimension=0...]
    all_to_all x0 -> x1, starting transfers between devices: none -> 5.6 us  [on_device(): lax.all_to_all(weight_term[:, split_cols:].reshape(fsdp_size, weight_rows...]
  transfers between devices with their start and end apart: 5 -> 6, of which waited for: 3 -> 4; matrix products, arithmetic and copies ran while one was open for 49% -> 49% of each run, Pallas kernels for 0% -> 0%
where the time goes in v3:
time: 287 us; the launch traced here: 286 us
  matrix products  88.6 us (31%)
  blocking collectives  56 us (20%)
  waiting for transfers between devices  45.7 us (16%)
  local copies, waits for them, and re-layouts  41.3 us (14%)
  other arithmetic  23.6 us (8%)
  starting transfers between devices  16.6 us (6%)
  between operations  14 us (5%)
    all_to_all x1, blocking collectives, on_device(): lax.all_to_all(value_term.reshape(fsdp_size, tok_rows, kv_width), 'fsdp',...  31.1 us
    all_gather x1, waiting for transfers between devices, on_device(): lax.all_gather(jnp.concatenate([keys, value_weight], axis=0), 'fsdp', axi...  28 us
    all_to_all x1, blocking collectives, on_device(): lax.all_to_all(frag_local[0].reshape(frag_rows, replicas, share_cols).tra...  24.9 us
    dot_general x1, matrix products, on_device(): jnp.einsum('tghd,sgd->ghts', grad_heads, value_groups, preferred_element_...  16.9 us
    dot_general x1, matrix products, on_device(): jnp.einsum('ghts,sgd->tghd', probs_low, value_groups, preferred_element_t...  16.7 us
    dot_general x1, matrix products, on_device(): jnp.einsum('ghts,tghd->sgd', probs_low, grad_heads, preferred_element_typ...  15.6 us
    dot_general x1, matrix products, on_device(): jnp.einsum('tghd,sgd->ghts', query_heads, key_groups, preferred_element_t...  15.3 us
    reduce_sum x1, other arithmetic, on_device(): summed = jnp.sum(jnp.exp(scores - top), axis=-1, keepdims=True)  14.5 us
  transfers between devices with their start and end apart: 6, of which 4 were waited for; matrix products, arithmetic and copies ran while one was open for 49% of the time, Pallas kernels for 0%

profile of v3, /device:TPU:1, one launch (start us, length us, event | category | flops | bytes accessed | tf_op | source)
XLA Modules:
  0.0 285.9 jit_solution(1303198870766476528)
XLA Ops:
  7.2 1.9 pad_maximum_fusion
  11.2 24.9 %all_to_all.25 = bf16[8,256,256]{2,1,0:T(8,128)(2,1)S(1)} all-to-all(bf16[8,256,256]{2,1,0:T(8,128)(2,1)S(1)} %copy.66), channel_id=1, replica_groups=mesh['replica'=8,'fsdp'=16] {'replica'}, dimensions={0} | all-to-all | bytes 2097152 | tf_op jit(solution)/shard_map/all_to_all | solution.py:38
  36.2 1.8 fusion.19
  39.1 3.6 %all-to-all-start.1 = ((bf16[8,256,256]{2,1,0:T(8,128)(2,1)}), bf16[8,256,256]{2,1,0:T(8,128)(2,1)S(1)}, u32[]{:S(2)}, u32[]{:S(2)}) async-start(bf16[8,256,256]{2,1,0:T(8,128)(2,1)} %broadcast_in_dim.34), calls=%async_computation.1 | async-start | bytes 2097152 | tf_op jit(solution)/shard_map/all_to_all | solution.py:49
  44.0 2.3 copy.108
  46.5 10.2 %all-to-all-done.1 = bf16[8,256,256]{2,1,0:T(8,128)(2,1)S(1)} async-done(((bf16[8,256,256]{2,1,0:T(8,128)(2,1)}), bf16[8,256,256]{2,1,0:T(8,128)(2,1)S(1)}, u32[]{:S(2)}, u32[]{:S(2)}) %all-to-all-start.1) | async-done | bytes 1048608 | tf_op jit(solution)/shard_map/all_to_all | solution.py:49
  57.9 28.0 %all-gather.6.cloned.1.call-done = bf16[6144,512]{1,0:T(8,128)(2,1)} async-done(((bf16[384,512]{1,0:T(8,128)(2,1)}), bf16[6144,512]{1,0:T(8,128)(2,1)}) %all-gather.6.cloned.1.call-update) | async-done | bytes 6291472 | tf_op jit(solution)/shard_map/all_gather | solution.py:30
  85.9 2.6 slice.16
  88.5 4.6 %slice.17 = bf16[16,128,512]{2,1,0:T(8,128)(2,1)} slice(bf16[16,384,512]{2,1,0:T(8,128)(2,1)} %bitcast.122), slice={[0:16], [0:128], [0:512]} | slice | bytes 4194304 | tf_op jit(solution)/shard_map/slice | solution.py:33
  93.1 2.0 fusion.10
  95.1 2.9 %copy.68 = bf16[2048,512]{0,1:T(8,128)(2,1)S(1)} copy(bf16[2048,512]{1,0:T(8,128)(2,1)} %bitcast.116) | data formatting | bytes 4194304 | tf_op jit(solution)/shard_map/optimization_barrier | solution.py:59
  98.1 15.3 %fusion.4 = (f32[4,8,128]{2,1,0:T(8,128)S(1)}, f32[4,2048,128,8]{2,1,3,0:T(8,128)}) fusion(pred[128,2048]{0,1:T(8,128)(4,1)S(1)} %iota_compare_fusion, bf16[2048,4,128,1]{0,2,3,1:T(8,128)(2,1)S(1)} %bitcast.109, bf16[128,4,8,128]{0,3,2,1:T(8,128)(2,1)} %bitcast.113), kind=kOutput, calls=%fused_computation.8 | convolution fusion | flops 2172645376 | bytes 36978688 | tf_op jit(solution)/shard_map/tghd,sgd->ghts/dot_general | solution.py:70
  113.4 14.5 %exponential_reduce_fusion = f32[4,8,128]{2,1,0:T(8,128)S(1)} fusion(f32[4,2048,128,8]{2,1,3,0:T(8,128)} %get-tuple-element.54, f32[4,8,128]{2,1,0:T(8,128)S(1)} %get-tuple-element.53, pred[128,2048]{0,1:T(8,128)(4,1)S(1)} %iota_compare_fusion), kind=kLoop, calls=%fused_computation.6 | loop fusion | flops 33550336 | bytes 33849344 | tf_op jit(solution)/shard_map/reduce_sum | solution.py:75
  128.0 15.6 %fusion.8 = bf16[2048,4,128]{2,0,1:T(8,128)(2,1)} fusion(bf16[128,4,8,128]{0,3,2,1:T(8,128)(2,1)S(1)} %bitcast.127, f32[4,2048,128,8]{2,1,3,0:T(8,128)} %get-tuple-element.54, f32[4,8,128]{2,1,0:T(8,128)S(1)} %log_add_fusion, pred[128,2048]{0,1:T(8,128)(4,1)S(1)} %iota_compare_fusion), kind=kOutput, calls=%fused_computation.17 | convolution fusion | flops 2182086656 | bytes 36978688 | tf_op jit(solution)/shard_map/ghts,tghd->sgd/dot_general | solution.py:80
  143.6 2.9 %copy.79 = bf16[2048,4,128]{0,2,1:T(8,128)(2,1)S(1)} copy(bf16[2048,4,128]{2,0,1:T(8,128)(2,1)} %fusion.8) | data formatting | bytes 4194304 | tf_op jit(solution)/shard_map/convert_element_type | solution.py:82
  147.7 31.1 %all_to_all.26 = bf16[16,128,512]{1,2,0:T(8,128)(2,1)S(1)} all-to-all(bf16[16,128,512]{1,2,0:T(8,128)(2,1)S(1)} %copy.80), channel_id=1, replica_groups=mesh['replica'=8,'fsdp'=16] {'fsdp'}, dimensions={0} | all-to-all | bytes 4194304 | tf_op jit(solution)/shard_map/all_to_all | solution.py:85
  180.4 1.8 fusion.20
  182.2 1.5 copy.112
  183.8 5.6 %all-to-all-start.4 = ((bf16[16,256,256]{1,2,0:T(8,128)(2,1)}), bf16[16,256,256]{1,2,0:T(8,128)(2,1)}, u32[]{:S(2)}, u32[]{:S(2)}) async-start(bf16[16,256,256]{1,2,0:T(8,128)(2,1)} %bitcast.108), calls=%async_computation.5 | async-start | bytes 4194304 | tf_op jit(solution)/shard_map/all_to_all | solution.py:124
  190.1 16.7 %multiply_reduce_fusion = (f32[128,4,8]{0,2,1:T(8,128)}, bf16[4,128,8,128]{3,1,2,0:T(8,128)(2,1)}) fusion(bf16[128,4,8,128]{0,3,2,1:T(8,128)(2,1)S(1)} %bitcast.128, bf16[2048,4,128,1]{0,2,3,1:T(8,128)(2,1)} %bitcast.132, f32[4,2048,128,8]{2,1,3,0:T(8,128)} %get-tuple-element.54, f32[4,8,128]{2,1,0:T(8,128)S(1)} %log_add_fusion, ...), kind=kOutput, calls=%fused_computation.19 | convolution fusion | flops 2183655424 | bytes 38043648 | tf_op jit(solution)/shard_map/ghts,sgd->tghd/dot_general | solution.py:90
  206.8 16.9 %fusion.2 = bf16[4,8,128,2048]{2,3,1,0:T(8,128)(2,1)S(1)} fusion(f32[4,2048,128,8]{2,1,3,0:T(8,128)} %get-tuple-element.54, bf16[2048,4,128,1]{0,2,3,1:T(8,128)(2,1)} %bitcast.133, bf16[128,4,8,128]{0,3,2,1:T(8,128)(2,1)} %bitcast.126, f32[4,8,128]{2,1,0:T(8,128)} %bitcast.134, f32[4,8,128]{2,1,0:T(8,128)} %copy-done.15, pred[128,2048]{0,1:T(8,128)(4,1)} %copy-done.6), kind=kOutput, calls=%fused_computation.3 | convolution fusion | flops 2206203904 | bytes 53772288 | tf_op jit(solution)/shard_map/tghd,sgd->ghts/dot_general | solution.py:93
  223.8 6.8 %bitcast_convert_fusion.1 = bf16[4,2048,128]{1,2,0:T(8,128)(2,1)} fusion(bf16[4,8,128,2048]{2,3,1,0:T(8,128)(2,1)S(1)} %fusion.2, bf16[128,4,8,128]{0,3,2,1:T(8,128)(2,1)S(1)} %bitcast.114), kind=kOutput, calls=%fused_computation.15 | convolution fusion | flops 2148532224 | bytes 19922944 | tf_op jit(solution)/shard_map/ghts,tghd->sgd/dot_general | solution.py:106
  230.7 4.1 %copy.82 = bf16[2048,512]{1,0:T(8,128)(2,1)} copy(bf16[2048,512]{0,1:T(8,128)(2,1)} %bitcast.115) | data formatting | bytes 4194304 | tf_op jit(solution)/shard_map/optimization_barrier | solution.py:111
  234.7 3.9 %copy.83 = bf16[16,128,512]{1,2,0:T(8,128)(2,1)} copy(bf16[16,128,512]{2,1,0:T(8,128)(2,1)} %bitcast.119) | data formatting | bytes 4194304 | tf_op jit(solution)/shard_map/reshape | solution.py:113
  238.6 7.3 %all-to-all-start.3 = ((bf16[16,128,512]{1,2,0:T(8,128)(2,1)}), bf16[16,128,512]{1,2,0:T(8,128)(2,1)}, u32[]{:S(2)}, u32[]{:S(2)}) async-start(bf16[16,128,512]{1,2,0:T(8,128)(2,1)} %copy.83), calls=%async_computation.3 | async-start | bytes 4194304 | tf_op jit(solution)/shard_map/all_to_all | solution.py:112
  247.4 2.3 copy.86
  249.7 9.4 %convolution_convert_fusion = bf16[4,128,8,128]{3,1,2,0:T(8,128)(2,1)} fusion(bf16[2048,4,128,1]{0,2,3,1:T(8,128)(2,1)S(1)} %bitcast.110, bf16[4,8,128,2048]{2,3,1,0:T(8,128)(2,1)} %copy-done.2), kind=kOutput, calls=%fused_computation.21 | convolution fusion | flops 2148007936 | bytes 19922944 | tf_op jit(solution)/shard_map/ghts,sgd->tghd/dot_general | solution.py:101
  259.0 2.3 copy.87
  261.3 1.9 convert_reduce_fusion
  263.2 4.7 %fusion.7 = bf16[1,128,4096]{2,1,0:T(8,128)(2,1)} fusion(bf16[128,512]{0,1:T(8,128)(2,1)S(1)} %copy-done.10, bf16[4096,512]{1,0:T(8,128)(2,1)} %bitcast.112), kind=kOutput, calls=%fused_computation.13 | convolution fusion | flops 537919488 | bytes 5373952 | tf_op jit(solution)/shard_map/dot_general | solution.py:133
  267.9 6.0 %reduce-scatter.2.cloned.1.call-done = bf16[256,256]{0,1:T(8,128)(2,1)} async-done(((bf16[4096,256]{0,1:T(8,128)(2,1)}), bf16[256,256]{0,1:T(8,128)(2,1)}) %reduce-scatter.2.cloned.1.call-update) | async-done | bytes 131088 | tf_op jit(solution)/shard_map/reduce_scatter | solution.py:121
  276.7 1.9 reduce_sum.64
  (59 shorter events, 14.6 us)
Async XLA Ops:
  7.2 86.0 %copy-start = (bf16[1,128,4096]{2,1,0:T(8,128)(2,1)S(1)}, bf16[1,128,4096]{2,1,0:T(8,128)(2,1)}, u32[]{:S(2)}) copy-start(bf16[1,128,4096]{2,1,0:T(8,128)(2,1)} %param.8) | copy-start | bytes 3145732
  7.2 29.0 %copy-start.14 = (f32[256,256]{1,0:T(8,128)S(1)}, f32[256,256]{1,0:T(8,128)}, u32[]{:S(2)}) copy-start(f32[256,256]{1,0:T(8,128)} %param.13) | copy-start | bytes 786436
  7.2 78.7 %all-gather.6.cloned.1.call-start = ((), (), s32[]{:S(2)}) async-start(), calls=%async_computation.8 | async-start | bytes 6684672 | tf_op jit(solution)/shard_map/all_gather | solution.py:30
  11.1 31.5 %copy-start.11 = (bf16[1,128,4096]{2,1,0:T(8,128)(2,1)S(1)}, bf16[1,128,4096]{2,1,0:T(8,128)(2,1)}, u32[]{:S(2)}) copy-start(bf16[1,128,4096]{2,1,0:T(8,128)(2,1)} %param.12) | copy-start | bytes 3145732
  39.1 17.6 %all-to-all-start.1 = ((bf16[8,256,256]{2,1,0:T(8,128)(2,1)}), bf16[8,256,256]{2,1,0:T(8,128)(2,1)S(1)}, u32[]{:S(2)}, u32[]{:S(2)}) async-start(bf16[8,256,256]{2,1,0:T(8,128)(2,1)} %broadcast_in_dim.34), calls=%async_computation.1 | async-start | bytes 2097152 | tf_op jit(solution)/shard_map/all_to_all | solution.py:49
  42.6 147.5 %all-gather.4.cloned.1.call-start = ((), (), s32[]{:S(2)}) async-start(), calls=%async_computation.6 | async-start | bytes 2228224 | tf_op jit(solution)/shard_map/all_gather | solution.py:62
  46.4 143.7 %copy-start.6 = (pred[128,2048]{0,1:T(8,128)(4,1)}, pred[128,2048]{0,1:T(8,128)(4,1)S(1)}, u32[]{:S(2)}) copy-start(pred[128,2048]{0,1:T(8,128)(4,1)S(1)} %iota_compare_fusion) | copy-start | bytes 786436
  88.5 4.6 %copy-start.5 = (bf16[16,256,512]{2,1,0:T(8,128)(2,1)}, bf16[16,256,512]{2,1,0:T(8,128)(2,1)S(1)}, u32[]{:S(2)}) copy-start(bf16[16,256,512]{2,1,0:T(8,128)(2,1)S(1)} %slice.16) | copy-start | bytes 12582916
  98.1 15.3 %copy-start.3 = (bf16[2048,512]{0,1:T(8,128)(2,1)}, bf16[2048,512]{0,1:T(8,128)(2,1)S(1)}, u32[]{:S(2)}) copy-start(bf16[2048,512]{0,1:T(8,128)(2,1)S(1)} %copy.68) | copy-start | bytes 6291460
  113.4 14.6 %copy-start.12 = (bf16[1,128,4096]{1,2,0:T(8,128)(2,1)S(1)}, bf16[1,128,4096]{1,2,0:T(8,128)(2,1)}, u32[]{:S(2)}) copy-start(bf16[1,128,4096]{1,2,0:T(8,128)(2,1)} %copy.72) | copy-start | bytes 3145732
  128.0 62.2 %copy-start.15 = (f32[4,8,128]{2,1,0:T(8,128)}, f32[4,8,128]{2,1,0:T(8,128)S(1)}, u32[]{:S(2)}) copy-start(f32[4,8,128]{2,1,0:T(8,128)S(1)} %log_add_fusion) | copy-start | bytes 49156
  179.1 4.6 %copy-start.9 = (bf16[128,512]{0,1:T(8,128)(2,1)}, bf16[128,512]{0,1:T(8,128)(2,1)S(1)}, u32[]{:S(2)}) copy-start(bf16[128,512]{0,1:T(8,128)(2,1)S(1)} %reduce_sum.63) | copy-start | bytes 393220
  180.4 9.7 %copy-start.13 = (bf16[1,128,4096]{1,2,0:T(8,128)(2,1)S(1)}, bf16[1,128,4096]{1,2,0:T(8,128)(2,1)}, u32[]{:S(2)}) copy-start(bf16[1,128,4096]{1,2,0:T(8,128)(2,1)} %copy.72) | copy-start | bytes 3145732
  183.8 54.9 %all-to-all-start.4 = ((bf16[16,256,256]{1,2,0:T(8,128)(2,1)}), bf16[16,256,256]{1,2,0:T(8,128)(2,1)}, u32[]{:S(2)}, u32[]{:S(2)}) async-start(bf16[16,256,256]{1,2,0:T(8,128)(2,1)} %bitcast.108), calls=%async_computation.5 | async-start | bytes 4194304 | tf_op jit(solution)/shard_map/all_to_all | solution.py:124
  189.4 84.4 %reduce-scatter.2.cloned.1.call-start = ((), (), s32[]{:S(2)}) async-start(), calls=%async_computation.7 | async-start | bytes 2228224 | tf_op jit(solution)/shard_map/reduce_scatter | solution.py:121
  206.8 16.9 %copy-start.7 = (bf16[1,128,4096]{1,2,0:T(8,128)(2,1)S(1)}, bf16[1,128,4096]{1,2,0:T(8,128)(2,1)}, u32[]{:S(2)}) copy-start(bf16[1,128,4096]{1,2,0:T(8,128)(2,1)} %copy.108) | copy-start | bytes 3145732
  223.8 6.9 %copy-start.2 = (bf16[4,8,128,2048]{2,3,1,0:T(8,128)(2,1)}, bf16[4,8,128,2048]{2,3,1,0:T(8,128)(2,1)S(1)}, u32[]{:S(2)}) copy-start(bf16[4,8,128,2048]{2,3,1,0:T(8,128)(2,1)S(1)} %fusion.2) | copy-start | bytes 50331652
  230.6 15.3 %copy-start.8 = (bf16[8,256,256]{1,2,0:T(8,128)(2,1)S(1)}, bf16[8,256,256]{1,2,0:T(8,128)(2,1)}, u32[]{:S(2)}) copy-start(bf16[8,256,256]{1,2,0:T(8,128)(2,1)} %copy.67) | copy-start | bytes 3145732
  230.7 19.0 %copy-start.4 = (bf16[2048,512]{0,1:T(8,128)(2,1)S(1)}, bf16[2048,512]{0,1:T(8,128)(2,1)}, u32[]{:S(2)}) copy-start(bf16[2048,512]{0,1:T(8,128)(2,1)} %copy-done.3) | copy-start | bytes 6291460
  238.6 38.0 %all-to-all-start.3 = ((bf16[16,128,512]{1,2,0:T(8,128)(2,1)}), bf16[16,128,512]{1,2,0:T(8,128)(2,1)}, u32[]{:S(2)}, u32[]{:S(2)}) async-start(bf16[16,128,512]{1,2,0:T(8,128)(2,1)} %copy.83), calls=%async_computation.3 | async-start | bytes 4194304 | tf_op jit(solution)/shard_map/all_to_all | solution.py:112
  249.7 13.5 %copy-start.10 = (bf16[128,512]{0,1:T(8,128)(2,1)S(1)}, bf16[128,512]{0,1:T(8,128)(2,1)}, u32[]{:S(2)}) copy-start(bf16[128,512]{0,1:T(8,128)(2,1)} %copy-done.9) | copy-start | bytes 393220
  249.7 29.7 %copy-start.1 = (bf16[1,128,4096]{2,1,0:T(8,128)(2,1)S(1)}, bf16[1,128,4096]{2,1,0:T(8,128)(2,1)}, u32[]{:S(2)}) copy-start(bf16[1,128,4096]{2,1,0:T(8,128)(2,1)} %param.8) | copy-start | bytes 3145732
Sparse Core Ops, SparseCore 0:
  11.0 74.8 all-gather.5
  95.2 47.8 all-gather.3
  194.1 79.6 reduce-scatter.1

commit v4 on v3

--- a/solution.py
+++ b/solution.py
@@ -117,12 +117,12 @@
         tokens, value_grad, (((0,), (0,)), ((), ())), preferred_element_type=jnp.float32
     )
     weight_term = (product * proj_scale).astype(jnp.bfloat16)
-    split_cols = weight_term.shape[1] // 2
+    split_cols = weight_term.shape[1] // 4
     weight_left = lax.psum_scatter(
         weight_term[:, :split_cols], "fsdp", scatter_dimension=0, tiled=True
     ).astype(jnp.float32)
     weight_parts = lax.all_to_all(
-        weight_term[:, split_cols:].reshape(fsdp_size, weight_rows, split_cols),
+        weight_term[:, split_cols:].reshape(fsdp_size, weight_rows, weight_term.shape[1] - split_cols),
         "fsdp",
         0,
         0,

time: 287 us -> 308 us (1.073)
  waiting for transfers between devices: 45.7 us -> 63.1 us
  local copies, waits for them, and re-layouts: 41.3 us -> 44.9 us
    reduce_scatter x1, waiting for transfers between devices: 5.95 us -> 24.2 us  [on_device(): lax.psum_scatter(weight_term[:, :split_cols], 'fsdp', scatter_dimension=0...]
  transfers between devices with their start and end apart: 6 -> 6, of which waited for: 4 -> 3; matrix products, arithmetic and copies ran while one was open for 49% -> 47% of each run, Pallas kernels for 0% -> 0%
where the time goes in v4:
time: 308 us; the launch traced here: 307 us
  matrix products  88.4 us (29%)
  waiting for transfers between devices  63.1 us (20%)
  blocking collectives  56 us (18%)
  local copies, waits for them, and re-layouts  44.9 us (15%)
  other arithmetic  24 us (8%)
  starting transfers between devices  16.6 us (5%)
  between operations  14 us (5%)
    all_to_all x1, blocking collectives, on_device(): lax.all_to_all(value_term.reshape(fsdp_size, tok_rows, kv_width), 'fsdp',...  31.1 us
    all_gather x1, waiting for transfers between devices, on_device(): lax.all_gather(jnp.concatenate([keys, value_weight], axis=0), 'fsdp', axi...  28 us
    all_to_all x1, blocking collectives, on_device(): lax.all_to_all(frag_local[0].reshape(frag_rows, replicas, share_cols).tra...  24.9 us
    reduce_scatter x1, waiting for transfers between devices, on_device(): lax.psum_scatter(weight_term[:, :split_cols], 'fsdp', scatter_dimension=0...  24.2 us
    dot_general x1, matrix products, on_device(): jnp.einsum('tghd,sgd->ghts', grad_heads, value_groups, preferred_element_...  16.7 us
    dot_general x1, matrix products, on_device(): jnp.einsum('ghts,sgd->tghd', probs_low, value_groups, preferred_element_t...  16.7 us
    dot_general x1, matrix products, on_device(): jnp.einsum('ghts,tghd->sgd', probs_low, grad_heads, preferred_element_typ...  15.6 us
    dot_general x1, matrix products, on_device(): jnp.einsum('tghd,sgd->ghts', query_heads, key_groups, preferred_element_t...  15.4 us
  transfers between devices with their start and end apart: 6, of which 3 were waited for; matrix products, arithmetic and copies ran while one was open for 47% of the time, Pallas kernels for 0%

profile of v4, /device:TPU:1, one launch (start us, length us, event | category | flops | bytes accessed | tf_op | source)
XLA Modules:
  0.0 307.0 jit_solution(17384134245182058665)
XLA Ops:
  7.2 1.9 pad_maximum_fusion
  11.2 24.9 %all_to_all.25 = bf16[8,256,256]{2,1,0:T(8,128)(2,1)S(1)} all-to-all(bf16[8,256,256]{2,1,0:T(8,128)(2,1)S(1)} %copy.67), channel_id=1, replica_groups=mesh['replica'=8,'fsdp'=16] {'replica'}, dimensions={0} | all-to-all | bytes 2097152 | tf_op jit(solution)/shard_map/all_to_all | solution.py:38
  36.2 1.8 fusion.19
  39.1 3.6 %all-to-all-start.1 = ((bf16[8,256,256]{2,1,0:T(8,128)(2,1)}), bf16[8,256,256]{2,1,0:T(8,128)(2,1)S(1)}, u32[]{:S(2)}, u32[]{:S(2)}) async-start(bf16[8,256,256]{2,1,0:T(8,128)(2,1)} %broadcast_in_dim.34), calls=%async_computation.1 | async-start | bytes 2097152 | tf_op jit(solution)/shard_map/all_to_all | solution.py:49
  44.0 2.3 copy.111
  46.5 10.2 %all-to-all-done.1 = bf16[8,256,256]{2,1,0:T(8,128)(2,1)S(1)} async-done(((bf16[8,256,256]{2,1,0:T(8,128)(2,1)}), bf16[8,256,256]{2,1,0:T(8,128)(2,1)S(1)}, u32[]{:S(2)}, u32[]{:S(2)}) %all-to-all-start.1) | async-done | bytes 1048608 | tf_op jit(solution)/shard_map/all_to_all | solution.py:49
  57.9 28.0 %all-gather.6.cloned.1.call-done = bf16[6144,512]{1,0:T(8,128)(2,1)} async-done(((bf16[384,512]{1,0:T(8,128)(2,1)}), bf16[6144,512]{1,0:T(8,128)(2,1)}) %all-gather.6.cloned.1.call-update) | async-done | bytes 6291472 | tf_op jit(solution)/shard_map/all_gather | solution.py:30
  85.9 2.6 slice.16
  88.5 4.6 %slice.17 = bf16[16,128,512]{2,1,0:T(8,128)(2,1)} slice(bf16[16,384,512]{2,1,0:T(8,128)(2,1)} %bitcast.123), slice={[0:16], [0:128], [0:512]} | slice | bytes 4194304 | tf_op jit(solution)/shard_map/slice | solution.py:33
  93.1 2.0 fusion.10
  95.1 2.9 copy.69
  98.1 15.4 %fusion.4 = (f32[4,8,128]{2,1,0:T(8,128)S(1)}, f32[4,2048,128,8]{2,1,3,0:T(8,128)}) fusion(pred[128,2048]{0,1:T(8,128)(4,1)S(1)} %iota_compare_fusion, bf16[2048,4,128,1]{0,2,3,1:T(8,128)(2,1)S(1)} %bitcast.109, bf16[128,4,8,128]{0,3,2,1:T(8,128)(2,1)} %bitcast.115), kind=kOutput, calls=%fused_computation.8 | convolution fusion | flops 2172645376 | bytes 36978688 | tf_op jit(solution)/shard_map/tghd,sgd->ghts/dot_general | solution.py:70
  113.4 14.5 %exponential_reduce_fusion = f32[4,8,128]{2,1,0:T(8,128)S(1)} fusion(f32[4,2048,128,8]{2,1,3,0:T(8,128)} %get-tuple-element.52, f32[4,8,128]{2,1,0:T(8,128)S(1)} %get-tuple-element.51, pred[128,2048]{0,1:T(8,128)(4,1)S(1)} %iota_compare_fusion), kind=kLoop, calls=%fused_computation.6 | loop fusion | flops 33550336 | bytes 33849344 | tf_op jit(solution)/shard_map/reduce_sum | solution.py:75
  128.0 15.6 %fusion.8 = bf16[2048,4,128]{2,0,1:T(8,128)(2,1)} fusion(bf16[128,4,8,128]{0,3,2,1:T(8,128)(2,1)S(1)} %bitcast.128, f32[4,2048,128,8]{2,1,3,0:T(8,128)} %get-tuple-element.52, f32[4,8,128]{2,1,0:T(8,128)S(1)} %log_add_fusion, pred[128,2048]{0,1:T(8,128)(4,1)S(1)} %iota_compare_fusion), kind=kOutput, calls=%fused_computation.18 | convolution fusion | flops 2182086656 | bytes 36978688 | tf_op jit(solution)/shard_map/ghts,tghd->sgd/dot_general | solution.py:80
  143.6 2.9 copy.80
  147.7 31.1 %all_to_all.26 = bf16[16,128,512]{1,2,0:T(8,128)(2,1)S(1)} all-to-all(bf16[16,128,512]{1,2,0:T(8,128)(2,1)S(1)} %copy.81), channel_id=1, replica_groups=mesh['replica'=8,'fsdp'=16] {'fsdp'}, dimensions={0} | all-to-all | bytes 4194304 | tf_op jit(solution)/shard_map/all_to_all | solution.py:85
  180.4 2.0 slice.19
  183.4 3.9 %copy.115 = bf16[48,16,8,256]{3,2,0,1:T(8,128)(2,1)} copy(bf16[48,16,8,256]{3,2,1,0:T(8,128)(2,1)} %bitcast.114) | data formatting | bytes 6291456 | tf_op jit(solution)/shard_map/reshape | solution.py:125
  187.3 5.7 %all-to-all-start.4 = ((bf16[16,256,384]{1,2,0:T(8,128)(2,1)}), bf16[16,256,384]{1,2,0:T(8,128)(2,1)}, u32[]{:S(2)}, u32[]{:S(2)}) async-start(bf16[16,256,384]{1,2,0:T(8,128)(2,1)} %bitcast.113), calls=%async_computation.5 | async-start | bytes 6291456 | tf_op jit(solution)/shard_map/all_to_all | solution.py:124
  193.8 16.7 %multiply_reduce_fusion = (f32[128,4,8]{0,2,1:T(8,128)}, bf16[4,128,8,128]{3,1,2,0:T(8,128)(2,1)}) fusion(bf16[128,4,8,128]{0,3,2,1:T(8,128)(2,1)S(1)} %bitcast.129, bf16[2048,4,128,1]{0,2,3,1:T(8,128)(2,1)} %bitcast.133, f32[4,2048,128,8]{2,1,3,0:T(8,128)} %get-tuple-element.52, f32[4,8,128]{2,1,0:T(8,128)S(1)} %log_add_fusion, ...), kind=kOutput, calls=%fused_computation.19 | convolution fusion | flops 2183655424 | bytes 38043648 | tf_op jit(solution)/shard_map/ghts,sgd->tghd/dot_general | solution.py:90
  210.5 16.7 %fusion.2 = bf16[4,8,128,2048]{2,3,1,0:T(8,128)(2,1)S(1)} fusion(f32[4,2048,128,8]{2,1,3,0:T(8,128)} %get-tuple-element.52, bf16[2048,4,128,1]{0,2,3,1:T(8,128)(2,1)} %bitcast.134, bf16[128,4,8,128]{0,3,2,1:T(8,128)(2,1)} %bitcast.127, f32[4,8,128]{2,1,0:T(8,128)} %bitcast.135, f32[4,8,128]{2,1,0:T(8,128)} %copy-done.15, pred[128,2048]{0,1:T(8,128)(4,1)} %copy-done.6), kind=kOutput, calls=%fused_computation.3 | convolution fusion | flops 2206203904 | bytes 53772288 | tf_op jit(solution)/shard_map/tghd,sgd->ghts/dot_general | solution.py:93
  227.3 6.8 %bitcast_convert_fusion.1 = bf16[4,2048,128]{1,2,0:T(8,128)(2,1)} fusion(bf16[4,8,128,2048]{2,3,1,0:T(8,128)(2,1)S(1)} %fusion.2, bf16[128,4,8,128]{0,3,2,1:T(8,128)(2,1)S(1)} %bitcast.116), kind=kOutput, calls=%fused_computation.16 | convolution fusion | flops 2148532224 | bytes 19922944 | tf_op jit(solution)/shard_map/ghts,tghd->sgd/dot_general | solution.py:106
  234.1 4.1 %copy.83 = bf16[2048,512]{1,0:T(8,128)(2,1)} copy(bf16[2048,512]{0,1:T(8,128)(2,1)} %bitcast.117) | data formatting | bytes 4194304 | tf_op jit(solution)/shard_map/optimization_barrier | solution.py:111
  238.2 3.9 %copy.84 = bf16[16,128,512]{1,2,0:T(8,128)(2,1)} copy(bf16[16,128,512]{2,1,0:T(8,128)(2,1)} %bitcast.121) | data formatting | bytes 4194304 | tf_op jit(solution)/shard_map/reshape | solution.py:113
  242.1 7.3 %all-to-all-start.3 = ((bf16[16,128,512]{1,2,0:T(8,128)(2,1)}), bf16[16,128,512]{1,2,0:T(8,128)(2,1)}, u32[]{:S(2)}, u32[]{:S(2)}) async-start(bf16[16,128,512]{1,2,0:T(8,128)(2,1)} %copy.84), calls=%async_computation.3 | async-start | bytes 4194304 | tf_op jit(solution)/shard_map/all_to_all | solution.py:112
  250.8 24.2 %reduce-scatter.2.cloned.1.call-done = bf16[256,128]{0,1:T(8,128)(2,1)} async-done(((bf16[4096,128]{0,1:T(8,128)(2,1)}), bf16[256,128]{0,1:T(8,128)(2,1)}) %reduce-scatter.2.cloned.1.call-update) | async-done | bytes 65552 | tf_op jit(solution)/shard_map/reduce_scatter | solution.py:121
  275.9 2.3 copy.88
  278.2 9.2 %convolution_convert_fusion = bf16[4,128,8,128]{3,1,2,0:T(8,128)(2,1)} fusion(bf16[2048,4,128,1]{0,2,3,1:T(8,128)(2,1)S(1)} %bitcast.110, bf16[4,8,128,2048]{2,3,1,0:T(8,128)(2,1)} %copy-done.2), kind=kOutput, calls=%fused_computation.21 | convolution fusion | flops 2148007936 | bytes 19922944 | tf_op jit(solution)/shard_map/ghts,sgd->tghd/dot_general | solution.py:101
  287.4 2.3 copy.89
  289.7 4.7 %fusion.7 = bf16[1,128,4096]{2,1,0:T(8,128)(2,1)} fusion(bf16[128,512]{0,1:T(8,128)(2,1)S(1)} %copy-done.10, bf16[4096,512]{1,0:T(8,128)(2,1)} %bitcast.112), kind=kOutput, calls=%fused_computation.14 | convolution fusion | flops 537919488 | bytes 5373952 | tf_op jit(solution)/shard_map/dot_general | solution.py:133
  294.4 2.4 convert_reduce_fusion
  297.8 1.9 reduce_sum.64
  (60 shorter events, 14.8 us)
Async XLA Ops:
  7.2 86.0 %copy-start = (bf16[1,128,4096]{2,1,0:T(8,128)(2,1)S(1)}, bf16[1,128,4096]{2,1,0:T(8,128)(2,1)}, u32[]{:S(2)}) copy-start(bf16[1,128,4096]{2,1,0:T(8,128)(2,1)} %param.8) | copy-start | bytes 3145732
  7.2 29.0 %copy-start.14 = (f32[256,256]{1,0:T(8,128)S(1)}, f32[256,256]{1,0:T(8,128)}, u32[]{:S(2)}) copy-start(f32[256,256]{1,0:T(8,128)} %param.13) | copy-start | bytes 786436
  7.2 78.7 %all-gather.6.cloned.1.call-start = ((), (), s32[]{:S(2)}) async-start(), calls=%async_computation.8 | async-start | bytes 6684672 | tf_op jit(solution)/shard_map/all_gather | solution.py:30
  11.1 31.5 %copy-start.11 = (bf16[1,128,4096]{2,1,0:T(8,128)(2,1)S(1)}, bf16[1,128,4096]{2,1,0:T(8,128)(2,1)}, u32[]{:S(2)}) copy-start(bf16[1,128,4096]{2,1,0:T(8,128)(2,1)} %param.12) | copy-start | bytes 3145732
  39.1 17.6 %all-to-all-start.1 = ((bf16[8,256,256]{2,1,0:T(8,128)(2,1)}), bf16[8,256,256]{2,1,0:T(8,128)(2,1)S(1)}, u32[]{:S(2)}, u32[]{:S(2)}) async-start(bf16[8,256,256]{2,1,0:T(8,128)(2,1)} %broadcast_in_dim.34), calls=%async_computation.1 | async-start | bytes 2097152 | tf_op jit(solution)/shard_map/all_to_all | solution.py:49
  42.6 151.1 %all-gather.4.cloned.1.call-start = ((), (), s32[]{:S(2)}) async-start(), calls=%async_computation.6 | async-start | bytes 2228224 | tf_op jit(solution)/shard_map/all_gather | solution.py:62
  46.4 147.3 %copy-start.6 = (pred[128,2048]{0,1:T(8,128)(4,1)}, pred[128,2048]{0,1:T(8,128)(4,1)S(1)}, u32[]{:S(2)}) copy-start(pred[128,2048]{0,1:T(8,128)(4,1)S(1)} %iota_compare_fusion) | copy-start | bytes 786436
  88.5 4.6 %copy-start.5 = (bf16[16,256,512]{2,1,0:T(8,128)(2,1)}, bf16[16,256,512]{2,1,0:T(8,128)(2,1)S(1)}, u32[]{:S(2)}) copy-start(bf16[16,256,512]{2,1,0:T(8,128)(2,1)S(1)} %slice.16) | copy-start | bytes 12582916
  98.1 15.4 %copy-start.3 = (bf16[2048,512]{0,1:T(8,128)(2,1)}, bf16[2048,512]{0,1:T(8,128)(2,1)S(1)}, u32[]{:S(2)}) copy-start(bf16[2048,512]{0,1:T(8,128)(2,1)S(1)} %copy.69) | copy-start | bytes 6291460
  113.4 14.6 %copy-start.12 = (bf16[1,128,4096]{1,2,0:T(8,128)(2,1)S(1)}, bf16[1,128,4096]{1,2,0:T(8,128)(2,1)}, u32[]{:S(2)}) copy-start(bf16[1,128,4096]{1,2,0:T(8,128)(2,1)} %copy.73) | copy-start | bytes 3145732
  128.0 65.8 %copy-start.15 = (f32[4,8,128]{2,1,0:T(8,128)}, f32[4,8,128]{2,1,0:T(8,128)S(1)}, u32[]{:S(2)}) copy-start(f32[4,8,128]{2,1,0:T(8,128)S(1)} %log_add_fusion) | copy-start | bytes 49156
  179.1 8.2 %copy-start.9 = (bf16[128,512]{0,1:T(8,128)(2,1)}, bf16[128,512]{0,1:T(8,128)(2,1)S(1)}, u32[]{:S(2)}) copy-start(bf16[128,512]{0,1:T(8,128)(2,1)S(1)} %reduce_sum.63) | copy-start | bytes 393220
  182.4 11.4 %copy-start.13 = (bf16[1,128,4096]{1,2,0:T(8,128)(2,1)S(1)}, bf16[1,128,4096]{1,2,0:T(8,128)(2,1)}, u32[]{:S(2)}) copy-start(bf16[1,128,4096]{1,2,0:T(8,128)(2,1)} %copy.73) | copy-start | bytes 3145732
  187.3 54.7 %all-to-all-start.4 = ((bf16[16,256,384]{1,2,0:T(8,128)(2,1)}), bf16[16,256,384]{1,2,0:T(8,128)(2,1)}, u32[]{:S(2)}, u32[]{:S(2)}) async-start(bf16[16,256,384]{1,2,0:T(8,128)(2,1)} %bitcast.113), calls=%async_computation.5 | async-start | bytes 6291456 | tf_op jit(solution)/shard_map/all_to_all | solution.py:124
  193.0 82.1 %reduce-scatter.2.cloned.1.call-start = ((), (), s32[]{:S(2)}) async-start(), calls=%async_computation.7 | async-start | bytes 1114112 | tf_op jit(solution)/shard_map/reduce_scatter | solution.py:121
  210.5 16.8 %copy-start.7 = (bf16[1,128,4096]{1,2,0:T(8,128)(2,1)S(1)}, bf16[1,128,4096]{1,2,0:T(8,128)(2,1)}, u32[]{:S(2)}) copy-start(bf16[1,128,4096]{1,2,0:T(8,128)(2,1)} %copy.111) | copy-start | bytes 3145732
  227.3 6.9 %copy-start.2 = (bf16[4,8,128,2048]{2,3,1,0:T(8,128)(2,1)}, bf16[4,8,128,2048]{2,3,1,0:T(8,128)(2,1)S(1)}, u32[]{:S(2)}) copy-start(bf16[4,8,128,2048]{2,3,1,0:T(8,128)(2,1)S(1)} %fusion.2) | copy-start | bytes 50331652
  234.1 15.3 %copy-start.8 = (bf16[8,256,256]{1,2,0:T(8,128)(2,1)S(1)}, bf16[8,256,256]{1,2,0:T(8,128)(2,1)}, u32[]{:S(2)}) copy-start(bf16[8,256,256]{1,2,0:T(8,128)(2,1)} %copy.68) | copy-start | bytes 3145732
  234.1 44.1 %copy-start.4 = (bf16[2048,512]{0,1:T(8,128)(2,1)S(1)}, bf16[2048,512]{0,1:T(8,128)(2,1)}, u32[]{:S(2)}) copy-start(bf16[2048,512]{0,1:T(8,128)(2,1)} %copy-done.3) | copy-start | bytes 6291460
  242.1 55.7 %all-to-all-start.3 = ((bf16[16,128,512]{1,2,0:T(8,128)(2,1)}), bf16[16,128,512]{1,2,0:T(8,128)(2,1)}, u32[]{:S(2)}, u32[]{:S(2)}) async-start(bf16[16,128,512]{1,2,0:T(8,128)(2,1)} %copy.84), calls=%async_computation.3 | async-start | bytes 4194304 | tf_op jit(solution)/shard_map/all_to_all | solution.py:112
  278.2 11.5 %copy-start.10 = (bf16[128,512]{0,1:T(8,128)(2,1)S(1)}, bf16[128,512]{0,1:T(8,128)(2,1)}, u32[]{:S(2)}) copy-start(bf16[128,512]{0,1:T(8,128)(2,1)} %copy-done.9) | copy-start | bytes 393220
  278.2 22.2 %copy-start.1 = (bf16[1,128,4096]{2,1,0:T(8,128)(2,1)S(1)}, bf16[1,128,4096]{2,1,0:T(8,128)(2,1)}, u32[]{:S(2)}) copy-start(bf16[1,128,4096]{2,1,0:T(8,128)(2,1)} %param.8) | copy-start | bytes 3145732
Sparse Core Ops, SparseCore 0:
  11.0 74.8 all-gather.5
  95.2 47.7 all-gather.3
  198.2 76.8 reduce-scatter.1

commit v5 on v3

--- a/solution.py
+++ b/solution.py
@@ -27,11 +27,14 @@
     key_rows = keys.shape[0]
     weight_rows = value_weight.shape[0]
     fsdp_size = lax.axis_size("fsdp")
-    gathered = lax.all_gather(
-        jnp.concatenate([keys, value_weight], axis=0), "fsdp", axis=0, tiled=False
-    )
-    keys_all = gathered[:, :key_rows].reshape(fsdp_size * key_rows, keys.shape[1])
-    weight_all = gathered[:, key_rows:].reshape(fsdp_size * weight_rows, value_weight.shape[1])
+    keys_all = lax.all_to_all(
+        jnp.broadcast_to(keys[None], (fsdp_size, key_rows, keys.shape[1])),
+        "fsdp",
+        0,
+        0,
+        tiled=True,
+    ).reshape(fsdp_size * key_rows, keys.shape[1])
+    weight_all = lax.all_gather(value_weight, "fsdp", axis=0, tiled=True)
     replicas = lax.axis_size("replica")
     share_cols = frag_global.shape[1]
     frag_rows = frag_global.shape[0]

time: 287 us -> 318 us (1.11)
  blocking collectives: 56 us -> 36.4 us
  starting transfers between devices: 16.6 us -> 32.1 us
  waiting for transfers between devices: 45.7 us -> 59.3 us
  matrix products: 88.6 us -> 100 us
  local copies, waits for them, and re-layouts: 41.3 us -> 51.8 us
    all_to_all x0 -> x2, waiting for transfers between devices: none -> 39.1 us  [the longest x1 25.3 us: on_device(): lax.all_to_all(jnp.broadcast_to(keys[None], (fsdp_size, key_rows, keys.sh...]
    all_gather x1, waiting for transfers between devices: 28 us -> 0.02 us  [on_device(): weight_all = lax.all_gather(value_weight, 'fsdp', axis=0, tiled=True)]
    all_to_all x1 -> x0, blocking collectives: 24.9 us -> none  [on_device(): lax.all_to_all(frag_local[0].reshape(frag_rows, replicas, share_cols).tra...]
    all_to_all x0 -> x2, starting transfers between devices: none -> 16.2 us  [the longest x1 9.33 us: on_device(): lax.all_to_all(jnp.broadcast_to(keys[None], (fsdp_size, key_rows, keys.sh...]
    reshape x0 -> x3, local copies, waits for them, and re-layouts: none -> 10.9 us  [the longest x2 6.93 us: on_device(): key_groups = keys_all.reshape(length_all, kv_heads, HD)]
    slice x2 -> x0, local copies, waits for them, and re-layouts: 7.21 us -> none  [the longest x1 4.6 us: on_device(): gathered[:, :key_rows].reshape(fsdp_size * key_rows, keys.shape[1])]
    dot_general x1, matrix products: 16.9 us -> 23.6 us  [on_device(): jnp.einsum('tghd,sgd->ghts', grad_heads, value_groups, preferred_element_...]
    reduce_scatter x1, waiting for transfers between devices: 5.95 us -> 0.02 us  [on_device(): lax.psum_scatter(weight_term[:, :split_cols], 'fsdp', scatter_dimension=0...]
  transfers between devices with their start and end apart: 6 -> 8, of which waited for: 4 -> 4; matrix products, arithmetic and copies ran while one was open for 49% -> 52% of each run, Pallas kernels for 0% -> 0%
where the time goes in v5:
time: 318 us; the launch traced here: 317 us
  matrix products  100 us (31%)
  waiting for transfers between devices  59.3 us (19%)
  local copies, waits for them, and re-layouts  51.8 us (16%)
  blocking collectives  36.4 us (11%)
  starting transfers between devices  32.1 us (10%)
  other arithmetic  23.3 us (7%)
  between operations  13.9 us (4%)
    all_to_all x1, blocking collectives, on_device(): lax.all_to_all(value_term.reshape(fsdp_size, tok_rows, kv_width), 'fsdp',...  36.4 us
    all_to_all x1, waiting for transfers between devices, on_device(): lax.all_to_all(jnp.broadcast_to(keys[None], (fsdp_size, key_rows, keys.sh...  25.3 us
    dot_general x1, matrix products, on_device(): jnp.einsum('tghd,sgd->ghts', grad_heads, value_groups, preferred_element_...  23.6 us
    dot_general x1, matrix products, on_device(): jnp.einsum('ghts,sgd->tghd', probs_low, value_groups, preferred_element_t...  16.9 us
    dot_general x1, matrix products, on_device(): jnp.einsum('ghts,tghd->sgd', probs_low, grad_heads, preferred_element_typ...  15.8 us
    dot_general x1, matrix products, on_device(): jnp.einsum('tghd,sgd->ghts', query_heads, key_groups, preferred_element_t...  14.5 us
    reduce_sum x1, other arithmetic, on_device(): summed = jnp.sum(jnp.exp(scores - top), axis=-1, keepdims=True)  14.4 us
    all_to_all x1, waiting for transfers between devices, on_device(): lax.all_to_all(jnp.broadcast_to(new_global.astype(jnp.bfloat16)[None], (r...  13.8 us
  transfers between devices with their start and end apart: 8, of which 4 were waited for; matrix products, arithmetic and copies ran while one was open for 52% of the time, Pallas kernels for 0%

profile of v5, /device:TPU:1, one launch (start us, length us, event | category | flops | bytes accessed | tf_op | source)
XLA Modules:
  0.0 317.1 jit_solution(1485866565581034788)
XLA Ops:
  10.1 6.9 %all-to-all-start = ((bf16[8,256,256]{2,1,0:T(8,128)(2,1)}), bf16[8,256,256]{2,1,0:T(8,128)(2,1)S(1)}, u32[]{:S(2)}, u32[]{:S(2)}) async-start(bf16[8,256,256]{2,1,0:T(8,128)(2,1)} %copy.69), calls=%async_computation | async-start | bytes 2097152 | tf_op jit(solution)/shard_map/all_to_all | solution.py:41
  17.7 13.8 %all-to-all-done = bf16[8,256,256]{2,1,0:T(8,128)(2,1)S(1)} async-done(((bf16[8,256,256]{2,1,0:T(8,128)(2,1)}), bf16[8,256,256]{2,1,0:T(8,128)(2,1)S(1)}, u32[]{:S(2)}, u32[]{:S(2)}) %all-to-all-start) | async-done | bytes 1048608 | tf_op jit(solution)/shard_map/all_to_all | solution.py:41
  34.6 4.1 %all-to-all-start.1 = ((bf16[8,256,256]{2,1,0:T(8,128)(2,1)}), bf16[8,256,256]{2,1,0:T(8,128)(2,1)S(1)}, u32[]{:S(2)}, u32[]{:S(2)}) async-start(bf16[8,256,256]{2,1,0:T(8,128)(2,1)} %broadcast_in_dim.41), calls=%async_computation.1 | async-start | bytes 2097152 | tf_op jit(solution)/shard_map/all_to_all | solution.py:52
  38.8 13.8 %all-to-all-done.1 = bf16[8,256,256]{2,1,0:T(8,128)(2,1)S(1)} async-done(((bf16[8,256,256]{2,1,0:T(8,128)(2,1)}), bf16[8,256,256]{2,1,0:T(8,128)(2,1)S(1)}, u32[]{:S(2)}, u32[]{:S(2)}) %all-to-all-start.1) | async-done | bytes 1048608 | tf_op jit(solution)/shard_map/all_to_all | solution.py:52
  54.4 9.3 %all-to-all-start.2 = ((bf16[16,128,512]{1,2,0:T(8,128)(2,1)}), bf16[16,128,512]{1,2,0:T(8,128)(2,1)S(1)}, u32[]{:S(2)}, u32[]{:S(2)}) async-start(bf16[16,128,512]{1,2,0:T(8,128)(2,1)} %broadcast_in_dim.43), calls=%async_computation.2 | async-start | bytes 4194304 | tf_op jit(solution)/shard_map/all_to_all | solution.py:30
  63.8 2.3 copy.77
  66.1 2.3 copy.118
  68.5 2.3 copy.70
  70.8 25.3 %all-to-all-done.2 = bf16[16,128,512]{1,2,0:T(8,128)(2,1)S(1)} async-done(((bf16[16,128,512]{1,2,0:T(8,128)(2,1)}), bf16[16,128,512]{1,2,0:T(8,128)(2,1)S(1)}, u32[]{:S(2)}, u32[]{:S(2)}) %all-to-all-start.2) | async-done | bytes 2097184 | tf_op jit(solution)/shard_map/all_to_all | solution.py:30
  96.1 2.6 copy.72
  98.7 4.0 %reshape.77 = bf16[2048,4,128]{2,1,0:T(4,128)(2,1)} reshape(bf16[2048,512]{1,0:T(8,128)(2,1)} %bitcast.95) | data formatting | bytes 4194304 | tf_op jit(solution)/shard_map/reshape | solution.py:71
  102.7 3.0 copy.102
  105.7 14.5 %fusion.4 = (f32[4,8,128]{2,1,0:T(8,128)S(1)}, f32[4,2048,128,8]{2,1,3,0:T(8,128)}) fusion(pred[128,2048]{0,1:T(8,128)(4,1)S(1)} %iota_compare_fusion, bf16[2048,4,128,1]{0,2,3,1:T(8,128)(2,1)S(1)} %copy.102, bf16[128,4,8,128]{0,3,2,1:T(8,128)(2,1)} %bitcast.91), kind=kOutput, calls=%fused_computation.8 | convolution fusion | flops 2172645376 | bytes 36978688 | tf_op jit(solution)/shard_map/tghd,sgd->ghts/dot_general | solution.py:73
  120.2 14.4 %exponential_reduce_fusion = f32[4,8,128]{2,1,0:T(8,128)S(1)} fusion(f32[4,2048,128,8]{2,1,3,0:T(8,128)} %get-tuple-element.54, f32[4,8,128]{2,1,0:T(8,128)S(1)} %get-tuple-element.53, pred[128,2048]{0,1:T(8,128)(4,1)S(1)} %iota_compare_fusion), kind=kLoop, calls=%fused_computation.6 | loop fusion | flops 33550336 | bytes 33849344 | tf_op jit(solution)/shard_map/reduce_sum | solution.py:78
  134.6 3.6 %fusion.15 = bf16[128,512]{1,0:T(8,128)(2,1)} fusion(bf16[4096,512]{1,0:T(8,128)(2,1)} %all-gather.3.cloned.1.call-done, bf16[1,128,4096]{2,1,0:T(8,128)(2,1)S(1)} %copy-done), kind=kOutput, calls=%fused_computation.27 | convolution fusion | flops 537001984 | bytes 5373952 | tf_op jit(solution)/shard_map/dot_general | solution.py:63
  138.2 15.8 %fusion.8 = bf16[2048,4,128]{2,0,1:T(8,128)(2,1)} fusion(bf16[128,4,8,128]{0,3,2,1:T(8,128)(2,1)} %bitcast.106, f32[4,2048,128,8]{2,1,3,0:T(8,128)} %get-tuple-element.54, f32[4,8,128]{2,1,0:T(8,128)S(1)} %log_add_fusion, pred[128,2048]{0,1:T(8,128)(4,1)S(1)} %iota_compare_fusion), kind=kOutput, calls=%fused_computation.17 | convolution fusion | flops 2182086656 | bytes 36978688 | tf_op jit(solution)/shard_map/ghts,tghd->sgd/dot_general | solution.py:83
  154.0 4.0 %copy.85 = bf16[2048,4,128]{0,2,1:T(8,128)(2,1)} copy(bf16[2048,4,128]{2,0,1:T(8,128)(2,1)} %fusion.8) | data formatting | bytes 4194304 | tf_op jit(solution)/shard_map/convert_element_type | solution.py:85
  158.0 2.2 copy.120
  160.8 36.4 %all_to_all.30 = bf16[16,128,512]{1,2,0:T(8,128)(2,1)} all-to-all(bf16[16,128,512]{1,2,0:T(8,128)(2,1)S(1)} %copy.86), channel_id=1, replica_groups=mesh['replica'=8,'fsdp'=16] {'fsdp'}, dimensions={0} | all-to-all | bytes 4194304 | tf_op jit(solution)/shard_map/all_to_all | solution.py:88
  203.7 4.5 %all-to-all-start.5 = ((bf16[16,256,256]{1,2,0:T(8,128)(2,1)}), bf16[16,256,256]{1,2,0:T(8,128)(2,1)}, u32[]{:S(2)}, u32[]{:S(2)}) async-start(bf16[16,256,256]{1,2,0:T(8,128)(2,1)} %bitcast.94), calls=%async_computation.6 | async-start | bytes 4194304 | tf_op jit(solution)/shard_map/all_to_all | solution.py:127
  208.9 3.9 %reshape.74 = bf16[2048,4,128]{2,1,0:T(4,128)(2,1)} reshape(bf16[2048,512]{1,0:T(8,128)(2,1)} %all-gather.5.cloned.1.call-done) | data formatting | bytes 4194304 | tf_op jit(solution)/shard_map/reshape | solution.py:92
  212.9 16.9 %multiply_reduce_fusion = (f32[128,4,8]{0,2,1:T(8,128)}, bf16[4,128,8,128]{3,1,2,0:T(8,128)(2,1)}) fusion(bf16[128,4,8,128]{0,3,2,1:T(8,128)(2,1)S(1)} %bitcast.108, f32[4,2048,128,8]{2,1,3,0:T(8,128)} %get-tuple-element.54, f32[4,8,128]{2,1,0:T(8,128)S(1)} %log_add_fusion, pred[128,2048]{0,1:T(8,128)(4,1)S(1)} %iota_compare_fusion, ...), kind=kOutput, calls=%fused_computation.19 | convolution fusion | flops 2183655424 | bytes 38043648 | tf_op jit(solution)/shard_map/ghts,sgd->tghd/dot_general | solution.py:93
  229.8 23.6 %fusion.2 = bf16[4,8,128,2048]{2,3,1,0:T(8,128)(2,1)} fusion(f32[4,2048,128,8]{2,1,3,0:T(8,128)} %get-tuple-element.54, bf16[128,4,8,128]{0,3,2,1:T(8,128)(2,1)} %bitcast.107, f32[4,8,128]{2,1,0:T(8,128)} %bitcast.112, f32[4,8,128]{2,1,0:T(8,128)S(1)} %log_add_fusion, pred[128,2048]{0,1:T(8,128)(4,1)S(1)} %iota_compare_fusion, ...), kind=kOutput, calls=%fused_computation.3 | convolution fusion | flops 2206203904 | bytes 53772288 | tf_op jit(solution)/shard_map/tghd,sgd->ghts/dot_general | solution.py:96
  253.4 10.7 %bitcast_convert_fusion.1 = bf16[4,2048,128]{1,2,0:T(8,128)(2,1)} fusion(bf16[4,8,128,2048]{2,3,1,0:T(8,128)(2,1)} %fusion.2, bf16[128,4,8,128]{0,3,2,1:T(8,128)(2,1)S(1)} %bitcast.92), kind=kOutput, calls=%fused_computation.15 | convolution fusion | flops 2148532224 | bytes 19922944 | tf_op jit(solution)/shard_map/ghts,tghd->sgd/dot_general | solution.py:109
  264.1 4.0 %copy.88 = bf16[2048,512]{1,0:T(8,128)(2,1)} copy(bf16[2048,512]{0,1:T(8,128)(2,1)} %bitcast.93) | data formatting | bytes 4194304 | tf_op jit(solution)/shard_map/optimization_barrier | solution.py:114
  268.2 3.9 %copy.89 = bf16[16,128,512]{1,2,0:T(8,128)(2,1)} copy(bf16[16,128,512]{2,1,0:T(8,128)(2,1)} %bitcast.99) | data formatting | bytes 4194304 | tf_op jit(solution)/shard_map/reshape | solution.py:116
  272.1 7.3 %all-to-all-start.4 = ((bf16[16,128,512]{1,2,0:T(8,128)(2,1)}), bf16[16,128,512]{1,2,0:T(8,128)(2,1)}, u32[]{:S(2)}, u32[]{:S(2)}) async-start(bf16[16,128,512]{1,2,0:T(8,128)(2,1)} %copy.89), calls=%async_computation.4 | async-start | bytes 4194304 | tf_op jit(solution)/shard_map/all_to_all | solution.py:115
  284.7 2.3 copy.92
  287.0 9.2 %convolution_convert_fusion = bf16[4,128,8,128]{3,1,2,0:T(8,128)(2,1)} fusion(bf16[2048,4,128,1]{0,2,3,1:T(8,128)(2,1)S(1)} %copy.102, bf16[4,8,128,2048]{2,3,1,0:T(8,128)(2,1)} %fusion.2), kind=kOutput, calls=%fused_computation.25 | convolution fusion | flops 2148007936 | bytes 19922944 | tf_op jit(solution)/shard_map/ghts,sgd->tghd/dot_general | solution.py:104
  296.2 2.3 copy.93
  298.5 4.7 %fusion.7 = bf16[1,128,4096]{2,1,0:T(8,128)(2,1)} fusion(bf16[128,512]{0,1:T(8,128)(2,1)S(1)} %reduce_sum.63, bf16[4096,512]{1,0:T(8,128)(2,1)} %all-gather.3.cloned.1.call-done), kind=kOutput, calls=%fused_computation.13 | convolution fusion | flops 537919488 | bytes 5373952 | tf_op jit(solution)/shard_map/dot_general | solution.py:136
  303.1 4.8 %all-to-all-done.4 = bf16[16,128,512]{1,2,0:T(8,128)(2,1)} async-done(((bf16[16,128,512]{1,2,0:T(8,128)(2,1)}), bf16[16,128,512]{1,2,0:T(8,128)(2,1)}, u32[]{:S(2)}, u32[]{:S(2)}) %all-to-all-start.4) | async-done | bytes 2097184 | tf_op jit(solution)/shard_map/all_to_all | solution.py:115
  (46 shorter events, 24.7 us)
Async XLA Ops:
  7.2 127.4 %copy-start = (bf16[1,128,4096]{2,1,0:T(8,128)(2,1)S(1)}, bf16[1,128,4096]{2,1,0:T(8,128)(2,1)}, u32[]{:S(2)}) copy-start(bf16[1,128,4096]{2,1,0:T(8,128)(2,1)} %param.8) | copy-start | bytes 3145732
  7.2 31.5 %copy-start.6 = (bf16[1,128,512]{2,1,0:T(8,128)(2,1)S(1)}, bf16[1,128,512]{2,1,0:T(8,128)(2,1)}, u32[]{:S(2)}) copy-start(bf16[1,128,512]{2,1,0:T(8,128)(2,1)} %param.10) | copy-start | bytes 393220
  10.1 21.4 %all-to-all-start = ((bf16[8,256,256]{2,1,0:T(8,128)(2,1)}), bf16[8,256,256]{2,1,0:T(8,128)(2,1)S(1)}, u32[]{:S(2)}, u32[]{:S(2)}) async-start(bf16[8,256,256]{2,1,0:T(8,128)(2,1)} %copy.69), calls=%async_computation | async-start | bytes 2097152 | tf_op jit(solution)/shard_map/all_to_all | solution.py:41
  17.0 117.6 %all-gather.3.cloned.1.call-start = ((), (), s32[]{:S(2)}) async-start(), calls=%async_computation.7 | async-start | bytes 4456448 | tf_op jit(solution)/shard_map/all_gather | solution.py:37
  34.6 18.0 %all-to-all-start.1 = ((bf16[8,256,256]{2,1,0:T(8,128)(2,1)}), bf16[8,256,256]{2,1,0:T(8,128)(2,1)S(1)}, u32[]{:S(2)}, u32[]{:S(2)}) async-start(bf16[8,256,256]{2,1,0:T(8,128)(2,1)} %broadcast_in_dim.41), calls=%async_computation.1 | async-start | bytes 2097152 | tf_op jit(solution)/shard_map/all_to_all | solution.py:52
  52.7 1.8 copy-start.4
  54.4 41.7 %all-to-all-start.2 = ((bf16[16,128,512]{1,2,0:T(8,128)(2,1)}), bf16[16,128,512]{1,2,0:T(8,128)(2,1)S(1)}, u32[]{:S(2)}, u32[]{:S(2)}) async-start(bf16[16,128,512]{1,2,0:T(8,128)(2,1)} %broadcast_in_dim.43), calls=%async_computation.2 | async-start | bytes 4194304 | tf_op jit(solution)/shard_map/all_to_all | solution.py:30
  63.8 145.2 %all-gather.5.cloned.1.call-start = ((), (), s32[]{:S(2)}) async-start(), calls=%async_computation.8 | async-start | bytes 2228224 | tf_op jit(solution)/shard_map/all_gather | solution.py:65
  202.1 10.8 %copy-start.5 = (bf16[1,128,4096]{1,2,0:T(8,128)(2,1)S(1)}, bf16[1,128,4096]{1,2,0:T(8,128)(2,1)}, u32[]{:S(2)}) copy-start(bf16[1,128,4096]{1,2,0:T(8,128)(2,1)} %copy.77) | copy-start | bytes 3145732
  203.7 68.4 %all-to-all-start.5 = ((bf16[16,256,256]{1,2,0:T(8,128)(2,1)}), bf16[16,256,256]{1,2,0:T(8,128)(2,1)}, u32[]{:S(2)}, u32[]{:S(2)}) async-start(bf16[16,256,256]{1,2,0:T(8,128)(2,1)} %bitcast.94), calls=%async_computation.6 | async-start | bytes 4194304 | tf_op jit(solution)/shard_map/all_to_all | solution.py:127
  208.2 74.5 %reduce-scatter.2.cloned.1.call-start = ((), (), s32[]{:S(2)}) async-start(), calls=%async_computation.9 | async-start | bytes 2228224 | tf_op jit(solution)/shard_map/reduce_scatter | solution.py:124
  229.8 23.6 %copy-start.2 = (bf16[1,128,4096]{1,2,0:T(8,128)(2,1)S(1)}, bf16[1,128,4096]{1,2,0:T(8,128)(2,1)}, u32[]{:S(2)}) copy-start(bf16[1,128,4096]{1,2,0:T(8,128)(2,1)} %copy.118) | copy-start | bytes 3145732
  264.1 15.2 %copy-start.3 = (bf16[8,256,256]{1,2,0:T(8,128)(2,1)S(1)}, bf16[8,256,256]{1,2,0:T(8,128)(2,1)}, u32[]{:S(2)}) copy-start(bf16[8,256,256]{1,2,0:T(8,128)(2,1)} %copy.70) | copy-start | bytes 3145732
  272.1 35.9 %all-to-all-start.4 = ((bf16[16,128,512]{1,2,0:T(8,128)(2,1)}), bf16[16,128,512]{1,2,0:T(8,128)(2,1)}, u32[]{:S(2)}, u32[]{:S(2)}) async-start(bf16[16,128,512]{1,2,0:T(8,128)(2,1)} %copy.89), calls=%async_computation.4 | async-start | bytes 4194304 | tf_op jit(solution)/shard_map/all_to_all | solution.py:115
  287.0 23.7 %copy-start.1 = (bf16[1,128,4096]{2,1,0:T(8,128)(2,1)S(1)}, bf16[1,128,4096]{2,1,0:T(8,128)(2,1)}, u32[]{:S(2)}) copy-start(bf16[1,128,4096]{2,1,0:T(8,128)(2,1)} %param.8) | copy-start | bytes 3145732
Sparse Core Ops, SparseCore 0:
  20.2 67.7 all-gather.2
  138.3 67.8 all-gather.4
  212.9 68.6 reduce-scatter.1

commit v6 on v4

--- a/solution.py
+++ b/solution.py
@@ -117,7 +117,7 @@
         tokens, value_grad, (((0,), (0,)), ((), ())), preferred_element_type=jnp.float32
     )
     weight_term = (product * proj_scale).astype(jnp.bfloat16)
-    split_cols = weight_term.shape[1] // 4
+    split_cols = weight_term.shape[1] * 3 // 4
     weight_left = lax.psum_scatter(
         weight_term[:, :split_cols], "fsdp", scatter_dimension=0, tiled=True
     ).astype(jnp.float32)

time: 308 us -> 295 us (0.958)
  waiting for transfers between devices: 63.1 us -> 47.4 us
  local copies, waits for them, and re-layouts: 44.9 us -> 48.9 us
    reduce_scatter x1, waiting for transfers between devices: 24.2 us -> 0.01 us  [on_device(): lax.psum_scatter(weight_term[:, :split_cols], 'fsdp', scatter_dimension=0...]
    all_to_all x1, waiting for transfers between devices: 0.01 us -> 9.41 us  [on_device(): lax.all_to_all(key_term.reshape(fsdp_size, tok_rows, kv_width), 'fsdp', 0...]
    unnamed x40 -> x34, local copies, waits for them, and re-layouts: 11.2 us -> 19 us
  transfers between devices with their start and end apart: 6 -> 6, of which waited for: 3 -> 3; matrix products, arithmetic and copies ran while one was open for 47% -> 48% of each run, Pallas kernels for 0% -> 0%
where the time goes in v6:
time: 295 us; the launch traced here: 294 us
  matrix products  88.6 us (30%)
  blocking collectives  55.7 us (19%)
  local copies, waits for them, and re-layouts  48.9 us (17%)
  waiting for transfers between devices  47.4 us (16%)
  other arithmetic  23.1 us (8%)
  starting transfers between devices  16.5 us (6%)
  between operations  14 us (5%)
    all_to_all x1, blocking collectives, on_device(): lax.all_to_all(value_term.reshape(fsdp_size, tok_rows, kv_width), 'fsdp',...  31.1 us
    all_gather x1, waiting for transfers between devices, on_device(): lax.all_gather(jnp.concatenate([keys, value_weight], axis=0), 'fsdp', axi...  28.6 us
    all_to_all x1, blocking collectives, on_device(): lax.all_to_all(frag_local[0].reshape(frag_rows, replicas, share_cols).tra...  24.6 us
    unnamed x34, local copies, waits for them, and re-layouts  19 us
    dot_general x1, matrix products, on_device(): jnp.einsum('tghd,sgd->ghts', grad_heads, value_groups, preferred_element_...  17.2 us
    dot_general x1, matrix products, on_device(): jnp.einsum('ghts,sgd->tghd', probs_low, value_groups, preferred_element_t...  16.7 us
    dot_general x1, matrix products, on_device(): jnp.einsum('ghts,tghd->sgd', probs_low, grad_heads, preferred_element_typ...  15.6 us
    dot_general x1, matrix products, on_device(): jnp.einsum('tghd,sgd->ghts', query_heads, key_groups, preferred_element_t...  15.3 us
  transfers between devices with their start and end apart: 6, of which 3 were waited for; matrix products, arithmetic and copies ran while one was open for 48% of the time, Pallas kernels for 0%

profile of v6, /device:TPU:1, one launch (start us, length us, event | category | flops | bytes accessed | tf_op | source)
XLA Modules:
  0.0 294.3 jit_solution(6071784640603565489)
XLA Ops:
  11.1 24.6 %all_to_all.25 = bf16[8,256,256]{2,1,0:T(8,128)(2,1)S(1)} all-to-all(bf16[8,256,256]{2,1,0:T(8,128)(2,1)S(1)} %copy.66), channel_id=1, replica_groups=mesh['replica'=8,'fsdp'=16] {'replica'}, dimensions={0} | all-to-all | bytes 2097152 | tf_op jit(solution)/shard_map/all_to_all | solution.py:38
  35.8 1.9 fusion.19
  38.8 3.6 %all-to-all-start.1 = ((bf16[8,256,256]{2,1,0:T(8,128)(2,1)}), bf16[8,256,256]{2,1,0:T(8,128)(2,1)S(1)}, u32[]{:S(2)}, u32[]{:S(2)}) async-start(bf16[8,256,256]{2,1,0:T(8,128)(2,1)} %broadcast_in_dim.34), calls=%async_computation.1 | async-start | bytes 2097152 | tf_op jit(solution)/shard_map/all_to_all | solution.py:49
  42.4 2.3 copy.72
  44.7 2.3 copy.108
  47.1 8.7 %all-to-all-done.1 = bf16[8,256,256]{2,1,0:T(8,128)(2,1)S(1)} async-done(((bf16[8,256,256]{2,1,0:T(8,128)(2,1)}), bf16[8,256,256]{2,1,0:T(8,128)(2,1)S(1)}, u32[]{:S(2)}, u32[]{:S(2)}) %all-to-all-start.1) | async-done | bytes 1048608 | tf_op jit(solution)/shard_map/all_to_all | solution.py:49
  57.1 28.6 %all-gather.6.cloned.1.call-done = bf16[6144,512]{1,0:T(8,128)(2,1)} async-done(((bf16[384,512]{1,0:T(8,128)(2,1)}), bf16[6144,512]{1,0:T(8,128)(2,1)}) %all-gather.6.cloned.1.call-update) | async-done | bytes 6291472 | tf_op jit(solution)/shard_map/all_gather | solution.py:30
  85.6 2.6 slice.16
  88.2 4.6 %slice.17 = bf16[16,128,512]{2,1,0:T(8,128)(2,1)} slice(bf16[16,384,512]{2,1,0:T(8,128)(2,1)} %bitcast.121), slice={[0:16], [0:128], [0:512]} | slice | bytes 4194304 | tf_op jit(solution)/shard_map/slice | solution.py:33
  92.8 2.0 fusion.10
  94.8 2.9 copy.68
  97.8 15.3 %fusion.4 = (f32[4,8,128]{2,1,0:T(8,128)S(1)}, f32[4,2048,128,8]{2,1,3,0:T(8,128)}) fusion(pred[128,2048]{0,1:T(8,128)(4,1)S(1)} %iota_compare_fusion, bf16[2048,4,128,1]{0,2,3,1:T(8,128)(2,1)S(1)} %bitcast.109, bf16[128,4,8,128]{0,3,2,1:T(8,128)(2,1)} %bitcast.113), kind=kOutput, calls=%fused_computation.8 | convolution fusion | flops 2172645376 | bytes 36978688 | tf_op jit(solution)/shard_map/tghd,sgd->ghts/dot_general | solution.py:70
  113.1 14.5 %exponential_reduce_fusion = f32[4,8,128]{2,1,0:T(8,128)S(1)} fusion(f32[4,2048,128,8]{2,1,3,0:T(8,128)} %get-tuple-element.52, f32[4,8,128]{2,1,0:T(8,128)S(1)} %get-tuple-element.51, pred[128,2048]{0,1:T(8,128)(4,1)S(1)} %iota_compare_fusion), kind=kLoop, calls=%fused_computation.6 | loop fusion | flops 33550336 | bytes 33849344 | tf_op jit(solution)/shard_map/reduce_sum | solution.py:75
  127.7 15.6 %fusion.8 = bf16[2048,4,128]{2,0,1:T(8,128)(2,1)} fusion(bf16[128,4,8,128]{0,3,2,1:T(8,128)(2,1)S(1)} %bitcast.127, f32[4,2048,128,8]{2,1,3,0:T(8,128)} %get-tuple-element.52, f32[4,8,128]{2,1,0:T(8,128)S(1)} %log_add_fusion, pred[128,2048]{0,1:T(8,128)(4,1)S(1)} %iota_compare_fusion), kind=kOutput, calls=%fused_computation.16 | convolution fusion | flops 2182086656 | bytes 36978688 | tf_op jit(solution)/shard_map/ghts,tghd->sgd/dot_general | solution.py:80
  143.3 2.9 copy.79
  147.4 31.1 %all_to_all.26 = bf16[16,128,512]{1,2,0:T(8,128)(2,1)S(1)} all-to-all(bf16[16,128,512]{1,2,0:T(8,128)(2,1)S(1)} %copy.80), channel_id=1, replica_groups=mesh['replica'=8,'fsdp'=16] {'fsdp'}, dimensions={0} | all-to-all | bytes 4194304 | tf_op jit(solution)/shard_map/all_to_all | solution.py:85
  180.2 2.0 slice.18
  183.2 5.5 %all-to-all-start.4 = ((bf16[16,256,128]{1,2,0:T(8,128)(2,1)}), bf16[16,256,128]{1,2,0:T(8,128)(2,1)}, u32[]{:S(2)}, u32[]{:S(2)}) async-start(bf16[16,256,128]{1,2,0:T(8,128)(2,1)} %bitcast.108), calls=%async_computation.5 | async-start | bytes 2097152 | tf_op jit(solution)/shard_map/all_to_all | solution.py:124
  189.5 16.7 %multiply_reduce_fusion = (f32[128,4,8]{0,2,1:T(8,128)}, bf16[4,128,8,128]{3,1,2,0:T(8,128)(2,1)}) fusion(bf16[128,4,8,128]{0,3,2,1:T(8,128)(2,1)S(1)} %bitcast.128, bf16[2048,4,128,1]{0,2,3,1:T(8,128)(2,1)} %bitcast.132, f32[4,2048,128,8]{2,1,3,0:T(8,128)} %get-tuple-element.52, f32[4,8,128]{2,1,0:T(8,128)S(1)} %log_add_fusion, ...), kind=kOutput, calls=%fused_computation.18 | convolution fusion | flops 2183655424 | bytes 38043648 | tf_op jit(solution)/shard_map/ghts,sgd->tghd/dot_general | solution.py:90
  206.2 17.2 %fusion.2 = bf16[4,8,128,2048]{2,3,1,0:T(8,128)(2,1)S(1)} fusion(f32[4,2048,128,8]{2,1,3,0:T(8,128)} %get-tuple-element.52, bf16[2048,4,128,1]{0,2,3,1:T(8,128)(2,1)} %bitcast.133, bf16[128,4,8,128]{0,3,2,1:T(8,128)(2,1)} %bitcast.126, f32[4,8,128]{2,1,0:T(8,128)} %bitcast.134, f32[4,8,128]{2,1,0:T(8,128)} %copy-done.12, pred[128,2048]{0,1:T(8,128)(4,1)} %copy-done.6), kind=kOutput, calls=%fused_computation.3 | convolution fusion | flops 2206203904 | bytes 53772288 | tf_op jit(solution)/shard_map/tghd,sgd->ghts/dot_general | solution.py:93
  223.4 5.9 %copy-done.2 = bf16[4,8,128,2048]{2,3,1,0:T(8,128)(2,1)} copy-done((bf16[4,8,128,2048]{2,3,1,0:T(8,128)(2,1)}, bf16[4,8,128,2048]{2,3,1,0:T(8,128)(2,1)S(1)}, u32[]{:S(2)}) %copy-start.2) | copy-done | bytes 16777240
  229.3 6.9 %bitcast_convert_fusion.1 = bf16[4,2048,128]{1,2,0:T(8,128)(2,1)} fusion(bf16[4,8,128,2048]{2,3,1,0:T(8,128)(2,1)S(1)} %fusion.2, bf16[128,4,8,128]{0,3,2,1:T(8,128)(2,1)S(1)} %bitcast.114), kind=kOutput, calls=%fused_computation.15 | convolution fusion | flops 2148532224 | bytes 19922944 | tf_op jit(solution)/shard_map/ghts,tghd->sgd/dot_general | solution.py:106
  236.2 4.1 %copy.82 = bf16[2048,512]{1,0:T(8,128)(2,1)} copy(bf16[2048,512]{0,1:T(8,128)(2,1)} %bitcast.115) | data formatting | bytes 4194304 | tf_op jit(solution)/shard_map/optimization_barrier | solution.py:111
  240.2 4.0 %copy.83 = bf16[16,128,512]{1,2,0:T(8,128)(2,1)} copy(bf16[16,128,512]{2,1,0:T(8,128)(2,1)} %bitcast.119) | data formatting | bytes 4194304 | tf_op jit(solution)/shard_map/reshape | solution.py:113
  244.2 7.4 %all-to-all-start.3 = ((bf16[16,128,512]{1,2,0:T(8,128)(2,1)}), bf16[16,128,512]{1,2,0:T(8,128)(2,1)}, u32[]{:S(2)}, u32[]{:S(2)}) async-start(bf16[16,128,512]{1,2,0:T(8,128)(2,1)} %copy.83), calls=%async_computation.3 | async-start | bytes 4194304 | tf_op jit(solution)/shard_map/all_to_all | solution.py:112
  251.6 2.3 copy.90
  255.2 2.4 copy.86
  257.6 9.2 %convolution_convert_fusion = bf16[4,128,8,128]{3,1,2,0:T(8,128)(2,1)} fusion(bf16[2048,4,128,1]{0,2,3,1:T(8,128)(2,1)S(1)} %bitcast.110, bf16[4,8,128,2048]{2,3,1,0:T(8,128)(2,1)} %copy-done.2), kind=kOutput, calls=%fused_computation.20 | convolution fusion | flops 2148007936 | bytes 19922944 | tf_op jit(solution)/shard_map/ghts,sgd->tghd/dot_general | solution.py:101
  266.7 2.3 copy.87
  269.0 4.7 %fusion.7 = bf16[1,128,4096]{2,1,0:T(8,128)(2,1)} fusion(bf16[128,512]{0,1:T(8,128)(2,1)S(1)} %copy-done.9, bf16[4096,512]{1,0:T(8,128)(2,1)} %bitcast.112), kind=kOutput, calls=%fused_computation.13 | convolution fusion | flops 537919488 | bytes 5373952 | tf_op jit(solution)/shard_map/dot_general | solution.py:133
  273.7 9.4 %all-to-all-done.3 = bf16[16,128,512]{1,2,0:T(8,128)(2,1)} async-done(((bf16[16,128,512]{1,2,0:T(8,128)(2,1)}), bf16[16,128,512]{1,2,0:T(8,128)(2,1)}, u32[]{:S(2)}, u32[]{:S(2)}) %all-to-all-start.3) | async-done | bytes 2097184 | tf_op jit(solution)/shard_map/all_to_all | solution.py:112
  283.1 1.9 reduce_sum.64
  (54 shorter events, 15.4 us)
Async XLA Ops:
  7.2 85.7 %copy-start = (bf16[1,128,4096]{2,1,0:T(8,128)(2,1)S(1)}, bf16[1,128,4096]{2,1,0:T(8,128)(2,1)}, u32[]{:S(2)}) copy-start(bf16[1,128,4096]{2,1,0:T(8,128)(2,1)} %param.8) | copy-start | bytes 3145732
  7.2 78.4 %all-gather.6.cloned.1.call-start = ((), (), s32[]{:S(2)}) async-start(), calls=%async_computation.8 | async-start | bytes 6684672 | tf_op jit(solution)/shard_map/all_gather | solution.py:30
  38.8 17.0 %all-to-all-start.1 = ((bf16[8,256,256]{2,1,0:T(8,128)(2,1)}), bf16[8,256,256]{2,1,0:T(8,128)(2,1)S(1)}, u32[]{:S(2)}, u32[]{:S(2)}) async-start(bf16[8,256,256]{2,1,0:T(8,128)(2,1)} %broadcast_in_dim.34), calls=%async_computation.1 | async-start | bytes 2097152 | tf_op jit(solution)/shard_map/all_to_all | solution.py:49
  42.3 147.1 %all-gather.4.cloned.1.call-start = ((), (), s32[]{:S(2)}) async-start(), calls=%async_computation.6 | async-start | bytes 2228224 | tf_op jit(solution)/shard_map/all_gather | solution.py:62
  47.1 142.4 %copy-start.6 = (pred[128,2048]{0,1:T(8,128)(4,1)}, pred[128,2048]{0,1:T(8,128)(4,1)S(1)}, u32[]{:S(2)}) copy-start(pred[128,2048]{0,1:T(8,128)(4,1)S(1)} %iota_compare_fusion) | copy-start | bytes 786436
  88.2 4.6 %copy-start.5 = (bf16[16,256,512]{2,1,0:T(8,128)(2,1)}, bf16[16,256,512]{2,1,0:T(8,128)(2,1)S(1)}, u32[]{:S(2)}) copy-start(bf16[16,256,512]{2,1,0:T(8,128)(2,1)S(1)} %slice.16) | copy-start | bytes 12582916
  97.8 15.3 %copy-start.3 = (bf16[2048,512]{0,1:T(8,128)(2,1)}, bf16[2048,512]{0,1:T(8,128)(2,1)S(1)}, u32[]{:S(2)}) copy-start(bf16[2048,512]{0,1:T(8,128)(2,1)S(1)} %copy.68) | copy-start | bytes 6291460
  113.1 14.6 %copy-start.10 = (bf16[1,128,4096]{1,2,0:T(8,128)(2,1)S(1)}, bf16[1,128,4096]{1,2,0:T(8,128)(2,1)}, u32[]{:S(2)}) copy-start(bf16[1,128,4096]{1,2,0:T(8,128)(2,1)} %copy.72) | copy-start | bytes 3145732
  127.6 61.8 %copy-start.12 = (f32[4,8,128]{2,1,0:T(8,128)}, f32[4,8,128]{2,1,0:T(8,128)S(1)}, u32[]{:S(2)}) copy-start(f32[4,8,128]{2,1,0:T(8,128)S(1)} %log_add_fusion) | copy-start | bytes 49156
  178.8 27.4 %copy-start.8 = (bf16[128,512]{0,1:T(8,128)(2,1)}, bf16[128,512]{0,1:T(8,128)(2,1)S(1)}, u32[]{:S(2)}) copy-start(bf16[128,512]{0,1:T(8,128)(2,1)S(1)} %reduce_sum.63) | copy-start | bytes 393220
  178.8 10.7 %copy-start.11 = (bf16[1,128,4096]{1,2,0:T(8,128)(2,1)S(1)}, bf16[1,128,4096]{1,2,0:T(8,128)(2,1)}, u32[]{:S(2)}) copy-start(bf16[1,128,4096]{1,2,0:T(8,128)(2,1)} %copy.72) | copy-start | bytes 3145732
  183.2 61.0 %all-to-all-start.4 = ((bf16[16,256,128]{1,2,0:T(8,128)(2,1)}), bf16[16,256,128]{1,2,0:T(8,128)(2,1)}, u32[]{:S(2)}, u32[]{:S(2)}) async-start(bf16[16,256,128]{1,2,0:T(8,128)(2,1)} %bitcast.108), calls=%async_computation.5 | async-start | bytes 2097152 | tf_op jit(solution)/shard_map/all_to_all | solution.py:124
  188.7 97.0 %reduce-scatter.2.cloned.1.call-start = ((), (), s32[]{:S(2)}) async-start(), calls=%async_computation.7 | async-start | bytes 3342336 | tf_op jit(solution)/shard_map/reduce_scatter | solution.py:121
  206.2 23.1 %copy-start.7 = (bf16[1,128,4096]{1,2,0:T(8,128)(2,1)S(1)}, bf16[1,128,4096]{1,2,0:T(8,128)(2,1)}, u32[]{:S(2)}) copy-start(bf16[1,128,4096]{1,2,0:T(8,128)(2,1)} %copy.108) | copy-start | bytes 3145732
  223.4 5.9 %copy-start.2 = (bf16[4,8,128,2048]{2,3,1,0:T(8,128)(2,1)}, bf16[4,8,128,2048]{2,3,1,0:T(8,128)(2,1)S(1)}, u32[]{:S(2)}) copy-start(bf16[4,8,128,2048]{2,3,1,0:T(8,128)(2,1)S(1)} %fusion.2) | copy-start | bytes 50331652
  236.2 21.4 %copy-start.4 = (bf16[2048,512]{0,1:T(8,128)(2,1)S(1)}, bf16[2048,512]{0,1:T(8,128)(2,1)}, u32[]{:S(2)}) copy-start(bf16[2048,512]{0,1:T(8,128)(2,1)} %copy-done.3) | copy-start | bytes 6291460
  244.2 24.8 %copy-start.9 = (bf16[128,512]{0,1:T(8,128)(2,1)S(1)}, bf16[128,512]{0,1:T(8,128)(2,1)}, u32[]{:S(2)}) copy-start(bf16[128,512]{0,1:T(8,128)(2,1)} %copy-done.8) | copy-start | bytes 393220
  244.2 38.9 %all-to-all-start.3 = ((bf16[16,128,512]{1,2,0:T(8,128)(2,1)}), bf16[16,128,512]{1,2,0:T(8,128)(2,1)}, u32[]{:S(2)}, u32[]{:S(2)}) async-start(bf16[16,128,512]{1,2,0:T(8,128)(2,1)} %copy.83), calls=%async_computation.3 | async-start | bytes 4194304 | tf_op jit(solution)/shard_map/all_to_all | solution.py:112
  255.2 32.5 %copy-start.1 = (bf16[1,128,4096]{2,1,0:T(8,128)(2,1)S(1)}, bf16[1,128,4096]{2,1,0:T(8,128)(2,1)}, u32[]{:S(2)}) copy-start(bf16[1,128,4096]{2,1,0:T(8,128)(2,1)} %param.8) | copy-start | bytes 3145732
Sparse Core Ops, SparseCore 0:
  11.0 74.5 all-gather.5
  94.9 47.7 all-gather.3
  193.5 90.7 reduce-scatter.1
